TPU v7x, 256 devices: a whole 4x4x8 slice. The times are simulated.
256 devices in a mesh: seq: 32 (over z, y_lo, core), mp: 8 (over y_hi, x).
Axes of the slice: x: 4, y: 4 (y_hi: 2, y_lo: 2; y = y_hi * 2 + y_lo), z: 8, core: 2. Of those that a mesh axis runs over, the one named last changes fastest.
Arguments:
- tokens: bfloat16 [12288, 3072], P('seq', 'mp'), may hold values from -6 to 6
- w_qkv: bfloat16 [3072, 3, 3072], P(None, None, 'mp'), may hold values from -1 to 1
- q_gain: float32 [128], replicated, may hold values from 0 to 5
- k_gain: float32 [128], replicated, may hold values from 0 to 5
- w_out: bfloat16 [3072, 3072], P('mp'), may hold values from -0.15625 to 0.15625
- neighbours: int32 [32, 6], replicated, may hold values from 0 to 31, as said below
- counts: int32 [32], replicated, may hold values from 1 to 6
Outputs:
- mixed: bfloat16 [12288, 3072], P('seq', 'mp')
Inputs may be any that keep to these rules, and one draw needn't show every extreme that they name: `neighbours`: each row lists distinct tiles, each within 4 tiles of the row's own tile counted cyclically modulo 32.
All inputs are finite; a program needn't handle non-finite values.
Results may differ from a plain program's by a relative error of at most 0.014.
Values may be sent and summed in bfloat16 or wider, within the bound.
No kernel may reach another device: no remote copies, remote signals or barrier semaphores. Data moves between devices by JAX's collectives and lax.ppermute only.
A program may use at most 128 MiB of HBM per device.

v0:
```python
import jax
import jax.numpy as jnp
from jax import lax
from jax.sharding import PartitionSpec as P

HD = 128
TILE = 384
REACH = 4
NB = 6


def passed_along(value, axis, steps):
    count = lax.axis_size(axis)
    pairs = [(source, (source + steps) % count) for source in range(count)]
    return lax.ppermute(value, axis, pairs)


def head_norm(projected, gain_vec):
    per_head = projected.reshape(projected.shape[0], -1, HD)
    factor = lax.rsqrt(jnp.mean(per_head * per_head, axis=-1, keepdims=True) + 1e-06)
    return (per_head * factor * gain_vec).astype(jnp.bfloat16)


def on_device(tokens, w_qkv, q_gain, k_gain, w_out, neighbours, counts):
    tok_rows = tokens.shape[0]
    columns = w_qkv.shape[2]
    heads_here = columns // HD
    tiles_here = tok_rows // TILE
    total_tiles = neighbours.shape[0]
    span_here = (REACH + tiles_here - 1) // tiles_here
    flat_w = w_qkv.reshape(w_qkv.shape[0], 3 * columns)
    projected = jnp.dot(
        lax.all_gather(tokens, "mp", axis=1, tiled=True), flat_w, preferred_element_type=jnp.float32
    )
    queries = head_norm(projected[:, :columns], q_gain)
    key_part = head_norm(projected[:, columns : 2 * columns], k_gain).reshape(tok_rows, columns)
    value_part = projected[:, 2 * columns :].astype(jnp.bfloat16)
    paired = jnp.stack([key_part, value_part])
    blocks = []
    for offset in range(-span_here, span_here + 1):
        if offset == 0:
            blocks.append(paired)
        else:
            blocks.append(passed_along(paired, "seq", -offset))
    window = jnp.concatenate(blocks, axis=1)
    window_tiles = (2 * span_here + 1) * tiles_here
    position = lax.axis_index("seq")
    first_tile = position * tiles_here - span_here * tiles_here
    listed = lax.dynamic_slice_in_dim(neighbours, position * tiles_here, tiles_here, 0)
    used_counts = lax.dynamic_slice_in_dim(counts, position * tiles_here, tiles_here, 0)
    relative = jnp.mod(listed - first_tile, total_tiles)
    slot_used = jnp.arange(NB, dtype=jnp.int32)[None, :] < used_counts[:, None]
    query_blocks = queries.reshape(tiles_here, TILE, heads_here, HD)
    factor = HD ** (-0.5)
    hits = (
        relative[:, :, None] == jnp.arange(window_tiles, dtype=jnp.int32)[None, None, :]
    ) & slot_used[:, :, None]
    tile_mask = jnp.any(hits, axis=1)
    key_mask = jnp.repeat(tile_mask, TILE, axis=1)
    near_keys = window[0].reshape(window_tiles * TILE, heads_here, HD)
    near_values = window[1].reshape(window_tiles * TILE, heads_here, HD)
    scores = (
        jnp.einsum("tqhd,khd->thqk", query_blocks, near_keys, preferred_element_type=jnp.float32)
        * factor
    )
    scores = jnp.where(key_mask[:, None, None, :], scores, -jnp.inf)
    highest = jnp.max(scores, axis=-1, keepdims=True)
    expo = jnp.exp(scores - highest)
    probs = (expo / jnp.sum(expo, axis=-1, keepdims=True)).astype(jnp.bfloat16)
    attended = jnp.einsum("thqk,khd->tqhd", probs, near_values, preferred_element_type=jnp.float32)
    attended = attended.astype(jnp.bfloat16).reshape(tok_rows, columns)
    mixed_t = lax.psum_scatter(
        lax.dot_general(
            w_out, attended, (((0,), (1,)), ((), ())), preferred_element_type=jnp.float32
        ).astype(jnp.bfloat16),
        "mp",
        scatter_dimension=0,
        tiled=True,
    ).astype(jnp.float32)
    return mixed_t.T.astype(jnp.bfloat16)


def solution(mesh):
    return jax.shard_map(
        on_device,
        mesh=mesh,
        in_specs=(P("seq", "mp"), P(None, None, "mp"), P(), P(), P("mp", None), P(), P()),
        out_specs=P("seq", "mp"),
        check_vma=False,
    )
```

profile of v0, /device:TPU:8, one launch (start us, length us, event | category | flops | bytes accessed | tf_op | source)
XLA Modules:
  0.0 287.1 jit_solution(6885400218139403413)
XLA Ops:
  7.3 10.3 %copy.31 = bf16[3072,3,384]{0,2,1:T(8,128)(2,1)} copy(bf16[3072,3,384]{2,0,1:T(8,128)(2,1)} %param.8) | data formatting | bytes 14155776 | tf_op args[1]
  17.6 58.7 %all-gather.2.cloned.1.call-done = bf16[384,3072]{1,0:T(8,128)(2,1)} async-done(((bf16[384,384]{1,0:T(8,128)(2,1)}), bf16[384,3072]{1,0:T(8,128)(2,1)}) %all-gather.2.cloned.1.call-update) | async-done | bytes 2359312 | tf_op jit(solution)/shard_map/all_gather | solution.py:33
  76.3 7.0 %fusion.21 = f32[384,1152]{1,0:T(8,128)S(1)} fusion(bf16[384,3072]{1,0:T(8,128)(2,1)} %all-gather.2.cloned.1.call-done, bf16[3072,1152]{0,1:T(8,128)(2,1)} %bitcast.63), kind=kOutput, calls=%fused_computation.47 | convolution fusion | flops 2717908992 | bytes 11206656 | tf_op jit(solution)/shard_map/dot_general | solution.py:32
  85.4 1.3 copy.32
  87.8 2.3 fusion.20
  91.1 1.6 collective-permute-start
  94.3 1.8 collective-permute-start.7
  96.2 1.3 collective-permute-start.3
  98.7 1.3 copy.36
  100.1 8.8 %collective-permute-done = bf16[2,384,384]{2,1,0:T(8,128)(2,1)} collective-permute-done((bf16[2,384,384]{2,1,0:T(8,128)(2,1)}, bf16[2,384,384]{2,1,0:T(8,128)(2,1)}, u32[]{:S(2)}, u32[]{:S(2)}) %collective-permute-start) | collective-permute-done | bytes 589856 | tf_op jit(solution)/shard_map/ppermute | solution.py:15
  110.0 9.3 %collective-permute-done.1 = bf16[2,384,384]{2,1,0:T(8,128)(2,1)} collective-permute-done((bf16[2,384,384]{2,1,0:T(8,128)(2,1)}, bf16[2,384,384]{2,1,0:T(8,128)(2,1)}, u32[]{:S(2)}, u32[]{:S(2)}) %collective-permute-start.1) | collective-permute-done | bytes 589856 | tf_op jit(solution)/shard_map/ppermute | solution.py:15
  120.5 18.5 %collective-permute-done.2 = bf16[2,384,384]{2,1,0:T(8,128)(2,1)} collective-permute-done((bf16[2,384,384]{2,1,0:T(8,128)(2,1)}, bf16[2,384,384]{2,1,0:T(8,128)(2,1)}, u32[]{:S(2)}, u32[]{:S(2)}) %collective-permute-start.2) | collective-permute-done | bytes 589856 | tf_op jit(solution)/shard_map/ppermute | solution.py:15
  139.0 3.9 %collective-permute-start.6 = (bf16[2,384,384]{2,1,0:T(8,128)(2,1)}, bf16[2,384,384]{2,1,0:T(8,128)(2,1)S(1)}, u32[]{:S(2)}, u32[]{:S(2)}) collective-permute-start(bf16[2,384,384]{2,1,0:T(8,128)(2,1)} %pad_maximum_fusion), channel_id=1, source_target_pairs={{0,232},{8,240},{16,248},{24,0},{32,8},{40,16},{48,24},{56,32},{64... | collective-permute-start | bytes 1769480 | tf_op jit(solution)/shard_map/ppermute | solution.py:15
  145.4 11.5 %collective-permute-done.5 = bf16[2,384,384]{2,1,0:T(8,128)(2,1)S(1)} collective-permute-done((bf16[2,384,384]{2,1,0:T(8,128)(2,1)}, bf16[2,384,384]{2,1,0:T(8,128)(2,1)S(1)}, u32[]{:S(2)}, u32[]{:S(2)}) %collective-permute-start.5) | collective-permute-done | bytes 589856 | tf_op jit(solution)/shard_map/ppermute | solution.py:15
  158.3 2.9 fusion.19
  161.2 4.5 %copy.35 = bf16[1,3456,384]{1,2,0:T(8,128)(2,1)} copy(bf16[1,3456,384]{2,1,0:T(8,128)(2,1)} %get-tuple-element.5) | data formatting | bytes 5308416 | tf_op jit(solution)/shard_map/slice | solution.py:60
  165.7 4.5 %copy.34 = bf16[1,3456,384]{1,2,0:T(8,128)(2,1)} copy(bf16[1,3456,384]{2,1,0:T(8,128)(2,1)} %get-tuple-element.6) | data formatting | bytes 5308416 | tf_op jit(solution)/shard_map/slice | solution.py:61
  170.3 5.7 %bitcast_reduce_fusion = (f32[3,384]{1,0:T(4,128)S(1)}, f32[3,3456,384]{2,1,0:T(8,128)S(1)}) fusion(pred[3456]{0:T(1024)(128)(4,1)S(1)} %broadcast_in_dim.13, bf16[3456,3,128]{0,2,1:T(8,128)(2,1)} %bitcast.62, f32[384,3,128]{0,2,1:T(8,128)S(1)} %bitcast.65, f32[128]{0:T(128)S(1)} %copy-done.3, f32[384,3]{0,1:T(4,128)S(1)} %add_rsqrt_fusion), kind=kOutput, calls=%fused_computation.1 | convolution fusion | flops 1031601024 | bytes 19182464 | tf_op jit(solution)/shard_map/tqhd,khd->thqk/dot_general | solution.py:63
  176.0 4.3 %fusion.1 = f32[3,384]{1,0:T(4,128)S(1)} fusion(f32[3,3456,384]{2,1,0:T(8,128)S(1)} %get-tuple-element.10, f32[3,384]{1,0:T(4,128)S(1)} %get-tuple-element.9, pred[3456]{0:T(1024)(128)(4,1)S(1)} %broadcast_in_dim.13), kind=kLoop, calls=%fused_computation.5 | loop fusion | flops 15924096 | bytes 15937920 | tf_op jit(solution)/shard_map/reduce_sum | solution.py:69
  180.3 4.7 %fusion.5 = bf16[3,128,384]{2,1,0:T(8,128)(2,1)S(1)} fusion(bf16[3456,3,128]{0,2,1:T(8,128)(2,1)S(1)} %bitcast.66, f32[3,384]{1,0:T(4,128)S(1)} %fusion.1, f32[3,384]{1,0:T(4,128)S(1)} %get-tuple-element.9, f32[3,3456,384]{2,1,0:T(8,128)S(1)} %get-tuple-element.10, pred[3456]{0:T(1024)(128)(4,1)S(1)} %broadcast_in_dim.13), kind=kOutput, calls=%fused_computation.10 | convolution fusion | flops 1039269888 | bytes 18887040 | tf_op jit(solution)/shard_map/thqk,khd->tqhd/dot_general | solution.py:70
  185.0 2.8 fusion.4
  187.9 4.3 %copy.43 = bf16[3072,384]{1,0:T(8,128)(2,1)} copy(bf16[3072,384]{0,1:T(8,128)(2,1)} %fusion.4) | data formatting | bytes 4718592
  192.2 86.3 %reduce-scatter.4.cloned.1.call-done = bf16[384,384]{1,0:T(8,128)(2,1)} async-done(((bf16[3072,384]{1,0:T(8,128)(2,1)}), bf16[384,384]{1,0:T(8,128)(2,1)}) %reduce-scatter.4.cloned.1.call-update) | async-done | bytes 294928
  278.4 1.8 copy.44
  (51 shorter events, 14.1 us)
Async XLA Ops:
  6.5 178.5 %copy-start = (bf16[384,3072]{1,0:T(8,128)(2,1)S(1)}, bf16[384,3072]{1,0:T(8,128)(2,1)}, u32[]{:S(2)}) copy-start(bf16[384,3072]{1,0:T(8,128)(2,1)} %param.11) | copy-start | bytes 7077892
  6.5 69.7 %all-gather.2.cloned.1.call-start = ((), (), s32[]{:S(2)}) async-start(), calls=%async_computation.1 | async-start | bytes 2654208 | tf_op jit(solution)/shard_map/all_gather | solution.py:33
  7.3 10.3 %copy-start.5 = (f32[128]{0:T(128)S(1)}, f32[128]{0:T(128)}, u32[]{:S(2)}) copy-start(f32[128]{0:T(128)} %param.10) | copy-start | bytes 1540
  7.3 271.2 %reduce-scatter.4.cloned.1.call-start = ((), (), s32[]{:S(2)}) async-start(), calls=%async_computation.2 | async-start | bytes 2654208
  83.2 1.2 copy-start.2
  83.2 9.4 %copy-start.6 = (s32[32]{0:T(128)S(1)}, s32[32]{0:T(128)}, u32[]{:S(2)}) copy-start(s32[32]{0:T(128)} %param.13) | copy-start | bytes 388
  83.3 10.0 %copy-start.4 = (s32[32,6]{0,1:T(8,128)S(1)}, s32[32,6]{0,1:T(8,128)}, u32[]{:S(2)}) copy-start(s32[32,6]{0,1:T(8,128)} %param.12) | copy-start | bytes 2308
  91.1 17.8 %collective-permute-start = (bf16[2,384,384]{2,1,0:T(8,128)(2,1)}, bf16[2,384,384]{2,1,0:T(8,128)(2,1)}, u32[]{:S(2)}, u32[]{:S(2)}) collective-permute-start(bf16[2,384,384]{2,1,0:T(8,128)(2,1)} %pad_maximum_fusion), channel_id=1, source_target_pairs={{0,32},{8,40},{16,48},{24,56},{32,64},{40,72},{48,80},{56,88},{64,... | collective-permute-start | bytes 1769480 | tf_op jit(solution)/shard_map/ppermute | solution.py:15
  94.1 25.3 %collective-permute-start.1 = (bf16[2,384,384]{2,1,0:T(8,128)(2,1)}, bf16[2,384,384]{2,1,0:T(8,128)(2,1)}, u32[]{:S(2)}, u32[]{:S(2)}) collective-permute-start(bf16[2,384,384]{2,1,0:T(8,128)(2,1)} %pad_maximum_fusion), channel_id=1, source_target_pairs={{0,24},{8,32},{16,40},{24,48},{32,56},{40,64},{48,72},{56,80},{64,... | collective-permute-start | bytes 1769480 | tf_op jit(solution)/shard_map/ppermute | solution.py:15
  94.3 62.8 %collective-permute-start.7 = (bf16[2,384,384]{2,1,0:T(8,128)(2,1)}, bf16[2,384,384]{2,1,0:T(8,128)(2,1)}, u32[]{:S(2)}, u32[]{:S(2)}) collective-permute-start(bf16[2,384,384]{2,1,0:T(8,128)(2,1)} %pad_maximum_fusion), channel_id=1, source_target_pairs={{0,224},{8,232},{16,240},{24,248},{32,0},{40,8},{48,16},{56,24},{6... | collective-permute-start | bytes 1769480 | tf_op jit(solution)/shard_map/ppermute | solution.py:15
  96.2 47.9 %collective-permute-start.3 = (bf16[2,384,384]{2,1,0:T(8,128)(2,1)}, bf16[2,384,384]{2,1,0:T(8,128)(2,1)}, u32[]{:S(2)}, u32[]{:S(2)}) collective-permute-start(bf16[2,384,384]{2,1,0:T(8,128)(2,1)} %pad_maximum_fusion), channel_id=1, source_target_pairs={{0,8},{8,16},{16,24},{24,32},{32,40},{40,48},{48,56},{56,64},{64,7... | collective-permute-start | bytes 1769480 | tf_op jit(solution)/shard_map/ppermute | solution.py:15
  97.5 41.5 %collective-permute-start.2 = (bf16[2,384,384]{2,1,0:T(8,128)(2,1)}, bf16[2,384,384]{2,1,0:T(8,128)(2,1)}, u32[]{:S(2)}, u32[]{:S(2)}) collective-permute-start(bf16[2,384,384]{2,1,0:T(8,128)(2,1)} %pad_maximum_fusion), channel_id=1, source_target_pairs={{0,16},{8,24},{16,32},{24,40},{32,48},{40,56},{48,64},{56,72},{64,... | collective-permute-start | bytes 1769480 | tf_op jit(solution)/shard_map/ppermute | solution.py:15
  108.9 36.4 %collective-permute-start.4 = (bf16[2,384,384]{2,1,0:T(8,128)(2,1)}, bf16[2,384,384]{2,1,0:T(8,128)(2,1)S(1)}, u32[]{:S(2)}, u32[]{:S(2)}) collective-permute-start(bf16[2,384,384]{2,1,0:T(8,128)(2,1)} %pad_maximum_fusion), channel_id=1, source_target_pairs={{0,248},{8,0},{16,8},{24,16},{32,24},{40,32},{48,40},{56,48},{64,5... | collective-permute-start | bytes 1769480 | tf_op jit(solution)/shard_map/ppermute | solution.py:15
  119.3 37.6 %collective-permute-start.5 = (bf16[2,384,384]{2,1,0:T(8,128)(2,1)}, bf16[2,384,384]{2,1,0:T(8,128)(2,1)S(1)}, u32[]{:S(2)}, u32[]{:S(2)}) collective-permute-start(bf16[2,384,384]{2,1,0:T(8,128)(2,1)} %pad_maximum_fusion), channel_id=1, source_target_pairs={{0,240},{8,248},{16,0},{24,8},{32,16},{40,24},{48,32},{56,40},{64,... | collective-permute-start | bytes 1769480 | tf_op jit(solution)/shard_map/ppermute | solution.py:15
  139.0 18.0 %collective-permute-start.6 = (bf16[2,384,384]{2,1,0:T(8,128)(2,1)}, bf16[2,384,384]{2,1,0:T(8,128)(2,1)S(1)}, u32[]{:S(2)}, u32[]{:S(2)}) collective-permute-start(bf16[2,384,384]{2,1,0:T(8,128)(2,1)} %pad_maximum_fusion), channel_id=1, source_target_pairs={{0,232},{8,240},{16,248},{24,0},{32,8},{40,16},{48,24},{56,32},{64... | collective-permute-start | bytes 1769480 | tf_op jit(solution)/shard_map/ppermute | solution.py:15
  161.2 9.1 %copy-start.3 = (f32[128]{0:T(128)S(1)}, f32[128]{0:T(128)}, u32[]{:S(2)}) copy-start(f32[128]{0:T(128)} %param.9) | copy-start | bytes 1540
  176.0 4.3 %copy-start.1 = (bf16[1,3456,384]{1,2,0:T(8,128)(2,1)S(1)}, bf16[1,3456,384]{1,2,0:T(8,128)(2,1)}, u32[]{:S(2)}) copy-start(bf16[1,3456,384]{1,2,0:T(8,128)(2,1)} %copy.34) | copy-start | bytes 7962628
Sparse Core Ops, SparseCore 0:
  9.8 66.4 all-gather.1
  192.3 86.0 reduce-scatter.3
where the time goes:
time: 289 us; the launch traced here: 287 us
  waiting for transfers between devices  194 us (67%)
  local copies, waits for them, and re-layouts  40 us (14%)
  matrix products  20.2 us (7%)
  between operations  13.6 us (5%)
  starting transfers between devices  9.91 us (3%)
  other arithmetic  9.58 us (3%)
    unnamed x3, waiting for transfers between devices  87 us
    all_gather x1, waiting for transfers between devices, on_device(): lax.all_gather(tokens, 'mp', axis=1, tiled=True)  58.7 us
    ppermute x8, waiting for transfers between devices, passed_along(): return lax.ppermute(value, axis, pairs)  48.1 us
    unnamed x24, local copies, waits for them, and re-layouts  22.5 us
    ppermute x8, starting transfers between devices, passed_along(): return lax.ppermute(value, axis, pairs)  9.86 us
    slice x2, local copies, waits for them, and re-layouts, on_device(): near_keys = window[0].reshape(window_tiles * TILE, heads_here, HD)  7.38 us
    dot_general x1, matrix products, on_device(): jnp.dot(lax.all_gather(tokens, 'mp', axis=1, tiled=True), flat_w, preferr...  6.96 us
  transfers between devices with their start and end apart: 10, of which 6 were waited for; matrix products, arithmetic and copies ran while one was open for 6% of the time, Pallas kernels for 0%

commit v1 on v0

--- a/solution.py
+++ b/solution.py
@@ -29,9 +29,21 @@
     total_tiles = neighbours.shape[0]
     span_here = (REACH + tiles_here - 1) // tiles_here
     flat_w = w_qkv.reshape(w_qkv.shape[0], 3 * columns)
+    feats = tokens.shape[1]
+    mp_count = lax.axis_size("mp")
+    mp_here = lax.axis_index("mp")
     projected = jnp.dot(
-        lax.all_gather(tokens, "mp", axis=1, tiled=True), flat_w, preferred_element_type=jnp.float32
+        tokens,
+        lax.dynamic_slice_in_dim(flat_w, mp_here * feats, feats, 0),
+        preferred_element_type=jnp.float32,
     )
+    for step in range(1, mp_count):
+        source = (mp_here - step) % mp_count
+        projected = projected + jnp.dot(
+            passed_along(tokens, "mp", step),
+            lax.dynamic_slice_in_dim(flat_w, source * feats, feats, 0),
+            preferred_element_type=jnp.float32,
+        )
     queries = head_norm(projected[:, :columns], q_gain)
     key_part = head_norm(projected[:, columns : 2 * columns], k_gain).reshape(tok_rows, columns)
     value_part = projected[:, 2 * columns :].astype(jnp.bfloat16)
@@ -69,15 +81,21 @@
     probs = (expo / jnp.sum(expo, axis=-1, keepdims=True)).astype(jnp.bfloat16)
     attended = jnp.einsum("thqk,khd->tqhd", probs, near_values, preferred_element_type=jnp.float32)
     attended = attended.astype(jnp.bfloat16).reshape(tok_rows, columns)
-    mixed_t = lax.psum_scatter(
-        lax.dot_general(
-            w_out, attended, (((0,), (1,)), ((), ())), preferred_element_type=jnp.float32
-        ).astype(jnp.bfloat16),
-        "mp",
-        scatter_dimension=0,
-        tiled=True,
-    ).astype(jnp.float32)
-    return mixed_t.T.astype(jnp.bfloat16)
+    out_cols = w_out.shape[1] // mp_count
+    total = jnp.dot(
+        attended,
+        lax.dynamic_slice_in_dim(w_out, mp_here * out_cols, out_cols, 1),
+        preferred_element_type=jnp.float32,
+    ).astype(jnp.bfloat16).astype(jnp.float32)
+    for step in range(1, mp_count):
+        target = (mp_here + step) % mp_count
+        term = jnp.dot(
+            attended,
+            lax.dynamic_slice_in_dim(w_out, target * out_cols, out_cols, 1),
+            preferred_element_type=jnp.float32,
+        ).astype(jnp.bfloat16)
+        total = total + passed_along(term, "mp", step).astype(jnp.float32)
+    return total.astype(jnp.bfloat16)
 
 
 def solution(mesh):

time: 289 us -> 168 us (0.58)
  waiting for transfers between devices: 194 us -> 46.8 us
  starting transfers between devices: 9.91 us -> 69.4 us
  local copies, waits for them, and re-layouts: 40 us -> 21.1 us
  between operations: 13.6 us -> 0.41 us
    unnamed x3 -> x0, waiting for transfers between devices: 87 us -> none
    ppermute x8 -> x22, starting transfers between devices: 9.86 us -> 69.4 us  [passed_along(): return lax.ppermute(value, axis, pairs)]
    all_gather x1 -> x0, waiting for transfers between devices: 58.7 us -> none  [on_device(): lax.all_gather(tokens, 'mp', axis=1, tiled=True)]
    slice x2 -> x1, local copies, waits for them, and re-layouts: 7.38 us -> 0.36 us  [on_device(): near_keys = window[0].reshape(window_tiles * TILE, heads_here, HD)]
    slice x2 -> x0, local copies, waits for them, and re-layouts: 5.84 us -> none  [the longest x1 4.55 us: on_device(): near_values = window[1].reshape(window_tiles * TILE, heads_here, HD)]
    unnamed x24, local copies, waits for them, and re-layouts: 22.5 us -> 18.2 us
    dot_general x2 -> x16, matrix products: 9.8 us -> 13.4 us  [the longest x7 7.5 us: on_device(): jnp.dot(passed_along(tokens, 'mp', step), lax.dynamic_slice_in_dim(flat_w...]
    ppermute x8 -> x22, waiting for transfers between devices: 48.1 us -> 46.8 us  [passed_along(): return lax.ppermute(value, axis, pairs)]
  transfers between devices with their start and end apart: 10 -> 22, of which waited for: 6 -> 9; matrix products, arithmetic and copies ran while one was open for 6% -> 18% of each run, Pallas kernels for 0% -> 0%
where the time goes in v1:
time: 168 us; the launch traced here: 167 us
  starting transfers between devices  69.4 us (41%)
  waiting for transfers between devices  46.8 us (28%)
  matrix products  21.9 us (13%)
  local copies, waits for them, and re-layouts  21.1 us (13%)
  other arithmetic  7.76 us (5%)
    ppermute x22, starting transfers between devices, passed_along(): return lax.ppermute(value, axis, pairs)  69.4 us
    ppermute x22, waiting for transfers between devices, passed_along(): return lax.ppermute(value, axis, pairs)  46.8 us
    unnamed x24, local copies, waits for them, and re-layouts  18.2 us
    dot_general x7, matrix products, on_device(): jnp.dot(passed_along(tokens, 'mp', step), lax.dynamic_slice_in_dim(flat_w...  7.5 us
    dot_general x1, matrix products, on_device(): jnp.einsum('thqk,khd->tqhd', probs, near_values, preferred_element_type=j...  4.7 us
    reduce_sum x1, other arithmetic, on_device(): probs = (expo / jnp.sum(expo, axis=-1, keepdims=True)).astype(jnp.bfloat16)  4.3 us
    dot_general x1, matrix products, on_device(): jnp.einsum('tqhd,khd->thqk', query_blocks, near_keys, preferred_element_t...  3.73 us
  transfers between devices with their start and end apart: 22, of which 9 were waited for; matrix products, arithmetic and copies ran while one was open for 18% of the time, Pallas kernels for 0%

profile of v1, /device:TPU:8, one launch (start us, length us, event | category | flops | bytes accessed | tf_op | source)
XLA Modules:
  0.0 167.4 jit_solution(6095881012199947465)
XLA Ops:
  0.0 4.5 %collective-permute-start.6 = (bf16[384,384]{1,0:T(8,128)(2,1)}, bf16[384,384]{1,0:T(8,128)(2,1)}, u32[]{:S(2)}, u32[]{:S(2)}) collective-permute-start(bf16[384,384]{1,0:T(8,128)(2,1)} %param.7), channel_id=1, source_target_pairs={{0,7},{1,0},{2,1},{3,2},{4,3},{5,4},{6,5},{7,6},{8,15},{9,8},{10,9... | collective-permute-start | bytes 884744 | tf_op jit(solution)/shard_map/ppermute | solution.py:15
  6.9 2.3 %collective-permute-start.3 = (bf16[384,384]{1,0:T(8,128)(2,1)}, bf16[384,384]{1,0:T(8,128)(2,1)S(1)}, u32[]{:S(2)}, u32[]{:S(2)}) collective-permute-start(bf16[384,384]{1,0:T(8,128)(2,1)} %param.7), channel_id=1, source_target_pairs={{0,4},{1,5},{2,6},{3,7},{4,0},{5,1},{6,2},{7,3},{8,12},{9,13},{10,... | collective-permute-start | bytes 884744 | tf_op jit(solution)/shard_map/ppermute | solution.py:15
  11.6 10.3 %copy.15 = bf16[3072,3,384]{0,2,1:T(8,128)(2,1)} copy(bf16[3072,3,384]{2,0,1:T(8,128)(2,1)} %param.8) | data formatting | bytes 14155776 | tf_op args[1]
  22.0 2.0 %fusion.26 = f32[1152,384]{1,0:T(8,128)S(1)} fusion(bf16[384,384]{1,0:T(8,128)(2,1)S(1)} %copy-done.4, bf16[3072,1152]{0,1:T(8,128)(2,1)} %bitcast.76, s32[]{:T(128)S(6)} %select_n.124), kind=kOutput, calls=%fused_computation.38 | convolution fusion | flops 339738624 | bytes 2949124 | tf_op jit(solution)/shard_map/dot_general | solution.py:35
  24.0 4.1 %collective-permute-done = bf16[384,384]{1,0:T(8,128)(2,1)} collective-permute-done((bf16[384,384]{1,0:T(8,128)(2,1)}, bf16[384,384]{1,0:T(8,128)(2,1)}, u32[]{:S(2)}, u32[]{:S(2)}) %collective-permute-start) | collective-permute-done | bytes 294944 | tf_op jit(solution)/shard_map/ppermute | solution.py:15
  28.1 5.3 %collective-permute-start.2 = (bf16[384,384]{1,0:T(8,128)(2,1)S(1)}, bf16[384,384]{1,0:T(8,128)(2,1)S(1)}, u32[]{:S(2)}, u32[]{:S(2)}) collective-permute-start(bf16[384,384]{1,0:T(8,128)(2,1)S(1)} %copy-done.4), channel_id=1, source_target_pairs={{0,3},{1,4},{2,5},{3,6},{4,7},{5,0},{6,1},{7,2},{8,11},{9,12},{10,... | collective-permute-start | bytes 884744 | tf_op jit(solution)/shard_map/ppermute | solution.py:15
  33.4 2.0 %convolution_add_fusion.1 = f32[1152,384]{1,0:T(8,128)S(1)} fusion(f32[1152,384]{1,0:T(8,128)S(1)} %fusion.26, bf16[384,384]{1,0:T(8,128)(2,1)} %collective-permute-done, bf16[3072,1152]{0,1:T(8,128)(2,1)} %bitcast.77, s32[]{:T(128)S(6)} %select_n.126), kind=kOutput, calls=%fused_computation.13 | convolution fusion | flops 340180992 | bytes 4718596 | tf_op jit(solution)/shard_map/dot_general | solution.py:42
  39.3 5.5 %collective-permute-done.2 = bf16[384,384]{1,0:T(8,128)(2,1)S(1)} collective-permute-done((bf16[384,384]{1,0:T(8,128)(2,1)S(1)}, bf16[384,384]{1,0:T(8,128)(2,1)S(1)}, u32[]{:S(2)}, u32[]{:S(2)}) %collective-permute-start.2) | collective-permute-done | bytes 294944 | tf_op jit(solution)/shard_map/ppermute | solution.py:15
  55.0 2.7 %collective-permute-start.9 = (bf16[2,384,384]{1,2,0:T(8,128)(2,1)}, bf16[2,384,384]{1,2,0:T(8,128)(2,1)}, u32[]{:S(2)}, u32[]{:S(2)}) collective-permute-start(bf16[2,384,384]{1,2,0:T(8,128)(2,1)} %pad_maximum_fusion), channel_id=1, source_target_pairs={{0,16},{8,24},{16,32},{24,40},{32,48},{40,56},{48,64},{56,72},{64,... | collective-permute-start | bytes 1769480 | tf_op jit(solution)/shard_map/ppermute | solution.py:15
  60.6 11.1 %collective-permute-done.7 = bf16[2,384,384]{1,2,0:T(8,128)(2,1)} collective-permute-done((bf16[2,384,384]{1,2,0:T(8,128)(2,1)}, bf16[2,384,384]{1,2,0:T(8,128)(2,1)}, u32[]{:S(2)}, u32[]{:S(2)}) %collective-permute-start.7) | collective-permute-done | bytes 589856 | tf_op jit(solution)/shard_map/ppermute | solution.py:15
  74.1 5.9 %collective-permute-done.8 = bf16[2,384,384]{1,2,0:T(8,128)(2,1)} collective-permute-done((bf16[2,384,384]{1,2,0:T(8,128)(2,1)}, bf16[2,384,384]{1,2,0:T(8,128)(2,1)}, u32[]{:S(2)}, u32[]{:S(2)}) %collective-permute-start.8) | collective-permute-done | bytes 589856 | tf_op jit(solution)/shard_map/ppermute | solution.py:15
  80.0 19.5 %collective-permute-start.13 = (bf16[2,384,384]{1,2,0:T(8,128)(2,1)}, bf16[2,384,384]{1,2,0:T(8,128)(2,1)S(1)}, u32[]{:S(2)}, u32[]{:S(2)}) collective-permute-start(bf16[2,384,384]{1,2,0:T(8,128)(2,1)} %pad_maximum_fusion), channel_id=1, source_target_pairs={{0,232},{8,240},{16,248},{24,0},{32,8},{40,16},{48,24},{56,32},{64... | collective-permute-start | bytes 1769480 | tf_op jit(solution)/shard_map/ppermute | solution.py:15
  100.6 5.7 %collective-permute-done.9 = bf16[2,384,384]{1,2,0:T(8,128)(2,1)} collective-permute-done((bf16[2,384,384]{1,2,0:T(8,128)(2,1)}, bf16[2,384,384]{1,2,0:T(8,128)(2,1)}, u32[]{:S(2)}, u32[]{:S(2)}) %collective-permute-start.9) | collective-permute-done | bytes 589856 | tf_op jit(solution)/shard_map/ppermute | solution.py:15
  106.4 5.5 %collective-permute-start.14 = (bf16[2,384,384]{1,2,0:T(8,128)(2,1)}, bf16[2,384,384]{1,2,0:T(8,128)(2,1)S(1)}, u32[]{:S(2)}, u32[]{:S(2)}) collective-permute-start(bf16[2,384,384]{1,2,0:T(8,128)(2,1)} %pad_maximum_fusion), channel_id=1, source_target_pairs={{0,224},{8,232},{16,240},{24,248},{32,0},{40,8},{48,16},{56,24},{6... | collective-permute-start | bytes 1769480 | tf_op jit(solution)/shard_map/ppermute | solution.py:15
  115.7 4.1 %collective-permute-done.14 = bf16[2,384,384]{1,2,0:T(8,128)(2,1)S(1)} collective-permute-done((bf16[2,384,384]{1,2,0:T(8,128)(2,1)}, bf16[2,384,384]{1,2,0:T(8,128)(2,1)S(1)}, u32[]{:S(2)}, u32[]{:S(2)}) %collective-permute-start.14) | collective-permute-done | bytes 589856 | tf_op jit(solution)/shard_map/ppermute | solution.py:15
  121.0 3.7 %bitcast_reduce_fusion = (f32[3,384]{1,0:T(4,128)S(1)}, f32[3,3456,384]{2,1,0:T(8,128)S(1)}) fusion(pred[3456]{0:T(1024)(128)(4,1)S(1)} %broadcast_in_dim.13, bf16[3456,3,128]{0,2,1:T(8,128)(2,1)S(1)} %bitcast.92, f32[384,3,128]{2,0,1:T(8,128)S(1)} %copy-done.3, f32[128]{0:T(128)S(1)} %copy-done.5, f32[384,3]{0,1:T(4,128)S(1)} %add_rsqrt_fusion), kind=kOutput, calls=%fused_computation.1 | convolution fusion | flops 1031601024 | bytes 19182464 | tf_op jit(solution)/shard_map/tqhd,khd->thqk/dot_general | solution.py:75
  124.7 4.3 %fusion.1 = f32[3,384]{1,0:T(4,128)S(1)} fusion(f32[3,3456,384]{2,1,0:T(8,128)S(1)} %get-tuple-element.10, f32[3,384]{1,0:T(4,128)S(1)} %get-tuple-element.9, pred[3456]{0:T(1024)(128)(4,1)S(1)} %broadcast_in_dim.13), kind=kLoop, calls=%fused_computation.5 | loop fusion | flops 15924096 | bytes 15937920 | tf_op jit(solution)/shard_map/reduce_sum | solution.py:81
  129.0 4.7 %fusion.11 = bf16[3,128,384]{2,1,0:T(8,128)(2,1)S(1)} fusion(bf16[3456,3,128]{0,2,1:T(8,128)(2,1)S(1)} %bitcast.95, f32[3,384]{1,0:T(4,128)S(1)} %fusion.1, f32[3,384]{1,0:T(4,128)S(1)} %get-tuple-element.9, f32[3,3456,384]{2,1,0:T(8,128)S(1)} %get-tuple-element.10, pred[3456]{0:T(1024)(128)(4,1)S(1)} %broadcast_in_dim.13), kind=kOutput, calls=%fused_computation.25 | convolution fusion | flops 1039269888 | bytes 18887040 | tf_op jit(solution)/shard_map/thqk,khd->tqhd/dot_general | solution.py:82
  136.0 2.7 %collective-permute-start.20 = (bf16[384,384]{1,0:T(8,128)(2,1)S(1)}, bf16[384,384]{1,0:T(8,128)(2,1)S(1)}, u32[]{:S(2)}, u32[]{:S(2)}) collective-permute-start(bf16[384,384]{1,0:T(8,128)(2,1)S(1)} %convolution_convert_fusion.1), channel_id=1, source_target_pairs={{0,6},{1,7},{2,0},{3,1},{4,2},{5,3},{6,4},{7,5},{8,14},{9,15},{10,... | collective-permute-start | bytes 884744 | tf_op jit(solution)/shard_map/ppermute | solution.py:15
  139.0 2.1 %collective-permute-start.19 = (bf16[384,384]{1,0:T(8,128)(2,1)S(1)}, bf16[384,384]{1,0:T(8,128)(2,1)S(1)}, u32[]{:S(2)}, u32[]{:S(2)}) collective-permute-start(bf16[384,384]{1,0:T(8,128)(2,1)S(1)} %convolution_convert_fusion.2), channel_id=1, source_target_pairs={{0,5},{1,6},{2,7},{3,0},{4,1},{5,2},{6,3},{7,4},{8,13},{9,14},{10,... | collective-permute-start | bytes 884744 | tf_op jit(solution)/shard_map/ppermute | solution.py:15
  142.6 3.3 %collective-permute-start.17 = (bf16[384,384]{1,0:T(8,128)(2,1)S(1)}, bf16[384,384]{1,0:T(8,128)(2,1)S(1)}, u32[]{:S(2)}, u32[]{:S(2)}) collective-permute-start(bf16[384,384]{1,0:T(8,128)(2,1)S(1)} %convolution_convert_fusion.4), channel_id=1, source_target_pairs={{0,3},{1,4},{2,5},{3,6},{4,7},{5,0},{6,1},{7,2},{8,11},{9,12},{10,... | collective-permute-start | bytes 884744 | tf_op jit(solution)/shard_map/ppermute | solution.py:15
  148.0 2.6 %collective-permute-start.16 = (bf16[384,384]{1,0:T(8,128)(2,1)S(1)}, bf16[384,384]{1,0:T(8,128)(2,1)S(1)}, u32[]{:S(2)}, u32[]{:S(2)}) collective-permute-start(bf16[384,384]{1,0:T(8,128)(2,1)S(1)} %convolution_convert_fusion.5), channel_id=1, source_target_pairs={{0,2},{1,3},{2,4},{3,5},{4,6},{5,7},{6,0},{7,1},{8,10},{9,11},{10,... | collective-permute-start | bytes 884744 | tf_op jit(solution)/shard_map/ppermute | solution.py:15
  150.6 7.5 %collective-permute-start.15 = (bf16[384,384]{1,0:T(8,128)(2,1)S(1)}, bf16[384,384]{1,0:T(8,128)(2,1)S(1)}, u32[]{:S(2)}, u32[]{:S(2)}) collective-permute-start(bf16[384,384]{1,0:T(8,128)(2,1)S(1)} %convolution_convert_fusion.6), channel_id=1, source_target_pairs={{0,1},{1,2},{2,3},{3,4},{4,5},{5,6},{6,7},{7,0},{8,9},{9,10},{10,1... | collective-permute-start | bytes 884744 | tf_op jit(solution)/shard_map/ppermute | solution.py:15
  158.1 8.0 %collective-permute-done.18 = bf16[384,384]{1,0:T(8,128)(2,1)S(1)} collective-permute-done((bf16[384,384]{1,0:T(8,128)(2,1)S(1)}, bf16[384,384]{1,0:T(8,128)(2,1)S(1)}, u32[]{:S(2)}, u32[]{:S(2)}) %collective-permute-start.18) | collective-permute-done | bytes 294944 | tf_op jit(solution)/shard_map/ppermute | solution.py:15
  (82 shorter events, 37.5 us)
Async XLA Ops:
  0.0 133.8 %copy-start = (bf16[384,3072]{1,0:T(8,128)(2,1)S(1)}, bf16[384,3072]{1,0:T(8,128)(2,1)}, u32[]{:S(2)}) copy-start(bf16[384,3072]{1,0:T(8,128)(2,1)} %param.11) | copy-start | bytes 7077892
  0.0 35.3 %collective-permute-start.6 = (bf16[384,384]{1,0:T(8,128)(2,1)}, bf16[384,384]{1,0:T(8,128)(2,1)}, u32[]{:S(2)}, u32[]{:S(2)}) collective-permute-start(bf16[384,384]{1,0:T(8,128)(2,1)} %param.7), channel_id=1, source_target_pairs={{0,7},{1,0},{2,1},{3,2},{4,3},{5,4},{6,5},{7,6},{8,15},{9,8},{10,9... | collective-permute-start | bytes 884744 | tf_op jit(solution)/shard_map/ppermute | solution.py:15
  4.5 32.6 %collective-permute-start.5 = (bf16[384,384]{1,0:T(8,128)(2,1)}, bf16[384,384]{1,0:T(8,128)(2,1)S(1)}, u32[]{:S(2)}, u32[]{:S(2)}) collective-permute-start(bf16[384,384]{1,0:T(8,128)(2,1)} %param.7), channel_id=1, source_target_pairs={{0,6},{1,7},{2,0},{3,1},{4,2},{5,3},{6,4},{7,5},{8,14},{9,15},{10,... | collective-permute-start | bytes 884744 | tf_op jit(solution)/shard_map/ppermute | solution.py:15
  5.3 32.6 %collective-permute-start.4 = (bf16[384,384]{1,0:T(8,128)(2,1)}, bf16[384,384]{1,0:T(8,128)(2,1)S(1)}, u32[]{:S(2)}, u32[]{:S(2)}) collective-permute-start(bf16[384,384]{1,0:T(8,128)(2,1)} %param.7), channel_id=1, source_target_pairs={{0,5},{1,6},{2,7},{3,0},{4,1},{5,2},{6,3},{7,4},{8,13},{9,14},{10,... | collective-permute-start | bytes 884744 | tf_op jit(solution)/shard_map/ppermute | solution.py:15
  6.9 31.7 %collective-permute-start.3 = (bf16[384,384]{1,0:T(8,128)(2,1)}, bf16[384,384]{1,0:T(8,128)(2,1)S(1)}, u32[]{:S(2)}, u32[]{:S(2)}) collective-permute-start(bf16[384,384]{1,0:T(8,128)(2,1)} %param.7), channel_id=1, source_target_pairs={{0,4},{1,5},{2,6},{3,7},{4,0},{5,1},{6,2},{7,3},{8,12},{9,13},{10,... | collective-permute-start | bytes 884744 | tf_op jit(solution)/shard_map/ppermute | solution.py:15
  9.1 18.9 %collective-permute-start = (bf16[384,384]{1,0:T(8,128)(2,1)}, bf16[384,384]{1,0:T(8,128)(2,1)}, u32[]{:S(2)}, u32[]{:S(2)}) collective-permute-start(bf16[384,384]{1,0:T(8,128)(2,1)} %param.7), channel_id=1, source_target_pairs={{0,1},{1,2},{2,3},{3,4},{4,5},{5,6},{6,7},{7,0},{8,9},{9,10},{10,1... | collective-permute-start | bytes 884744 | tf_op jit(solution)/shard_map/ppermute | solution.py:15
  22.0 13.5 %copy-start.1 = (bf16[3072,3,384]{0,2,1:T(8,128)(2,1)S(1)}, bf16[3072,3,384]{0,2,1:T(8,128)(2,1)}, u32[]{:S(2)}) copy-start(bf16[3072,3,384]{0,2,1:T(8,128)(2,1)} %copy.15) | copy-start | bytes 21233668
  28.1 16.8 %collective-permute-start.2 = (bf16[384,384]{1,0:T(8,128)(2,1)S(1)}, bf16[384,384]{1,0:T(8,128)(2,1)S(1)}, u32[]{:S(2)}, u32[]{:S(2)}) collective-permute-start(bf16[384,384]{1,0:T(8,128)(2,1)S(1)} %copy-done.4), channel_id=1, source_target_pairs={{0,3},{1,4},{2,5},{3,6},{4,7},{5,0},{6,1},{7,2},{8,11},{9,12},{10,... | collective-permute-start | bytes 884744 | tf_op jit(solution)/shard_map/ppermute | solution.py:15
  35.3 11.3 %collective-permute-start.1 = (bf16[384,384]{1,0:T(8,128)(2,1)S(1)}, bf16[384,384]{1,0:T(8,128)(2,1)S(1)}, u32[]{:S(2)}, u32[]{:S(2)}) collective-permute-start(bf16[384,384]{1,0:T(8,128)(2,1)S(1)} %copy-done.4), channel_id=1, source_target_pairs={{0,2},{1,3},{2,4},{3,5},{4,6},{5,7},{6,0},{7,1},{8,10},{9,11},{10,... | collective-permute-start | bytes 884744 | tf_op jit(solution)/shard_map/ppermute | solution.py:15
  51.3 20.4 %collective-permute-start.7 = (bf16[2,384,384]{1,2,0:T(8,128)(2,1)}, bf16[2,384,384]{1,2,0:T(8,128)(2,1)}, u32[]{:S(2)}, u32[]{:S(2)}) collective-permute-start(bf16[2,384,384]{1,2,0:T(8,128)(2,1)} %pad_maximum_fusion), channel_id=1, source_target_pairs={{0,32},{8,40},{16,48},{24,56},{32,64},{40,72},{48,80},{56,88},{64,... | collective-permute-start | bytes 1769480 | tf_op jit(solution)/shard_map/ppermute | solution.py:15
  54.7 25.3 %collective-permute-start.8 = (bf16[2,384,384]{1,2,0:T(8,128)(2,1)}, bf16[2,384,384]{1,2,0:T(8,128)(2,1)}, u32[]{:S(2)}, u32[]{:S(2)}) collective-permute-start(bf16[2,384,384]{1,2,0:T(8,128)(2,1)} %pad_maximum_fusion), channel_id=1, source_target_pairs={{0,24},{8,32},{16,40},{24,48},{32,56},{40,64},{48,72},{56,80},{64,... | collective-permute-start | bytes 1769480 | tf_op jit(solution)/shard_map/ppermute | solution.py:15
  55.0 51.3 %collective-permute-start.9 = (bf16[2,384,384]{1,2,0:T(8,128)(2,1)}, bf16[2,384,384]{1,2,0:T(8,128)(2,1)}, u32[]{:S(2)}, u32[]{:S(2)}) collective-permute-start(bf16[2,384,384]{1,2,0:T(8,128)(2,1)} %pad_maximum_fusion), channel_id=1, source_target_pairs={{0,16},{8,24},{16,32},{24,40},{32,48},{40,56},{48,64},{56,72},{64,... | collective-permute-start | bytes 1769480 | tf_op jit(solution)/shard_map/ppermute | solution.py:15
  57.7 55.3 %collective-permute-start.10 = (bf16[2,384,384]{1,2,0:T(8,128)(2,1)}, bf16[2,384,384]{1,2,0:T(8,128)(2,1)}, u32[]{:S(2)}, u32[]{:S(2)}) collective-permute-start(bf16[2,384,384]{1,2,0:T(8,128)(2,1)} %pad_maximum_fusion), channel_id=1, source_target_pairs={{0,8},{8,16},{16,24},{24,32},{32,40},{40,48},{48,56},{56,64},{64,7... | collective-permute-start | bytes 1769480 | tf_op jit(solution)/shard_map/ppermute | solution.py:15
  59.5 54.9 %collective-permute-start.11 = (bf16[2,384,384]{1,2,0:T(8,128)(2,1)}, bf16[2,384,384]{1,2,0:T(8,128)(2,1)}, u32[]{:S(2)}, u32[]{:S(2)}) collective-permute-start(bf16[2,384,384]{1,2,0:T(8,128)(2,1)} %pad_maximum_fusion), channel_id=1, source_target_pairs={{0,248},{8,0},{16,8},{24,16},{32,24},{40,32},{48,40},{56,48},{64,5... | collective-permute-start | bytes 1769480 | tf_op jit(solution)/shard_map/ppermute | solution.py:15
  71.7 43.8 %collective-permute-start.12 = (bf16[2,384,384]{1,2,0:T(8,128)(2,1)}, bf16[2,384,384]{1,2,0:T(8,128)(2,1)S(1)}, u32[]{:S(2)}, u32[]{:S(2)}) collective-permute-start(bf16[2,384,384]{1,2,0:T(8,128)(2,1)} %pad_maximum_fusion), channel_id=1, source_target_pairs={{0,240},{8,248},{16,0},{24,8},{32,16},{40,24},{48,32},{56,40},{64,... | collective-permute-start | bytes 1769480 | tf_op jit(solution)/shard_map/ppermute | solution.py:15
  80.0 35.7 %collective-permute-start.13 = (bf16[2,384,384]{1,2,0:T(8,128)(2,1)}, bf16[2,384,384]{1,2,0:T(8,128)(2,1)S(1)}, u32[]{:S(2)}, u32[]{:S(2)}) collective-permute-start(bf16[2,384,384]{1,2,0:T(8,128)(2,1)} %pad_maximum_fusion), channel_id=1, source_target_pairs={{0,232},{8,240},{16,248},{24,0},{32,8},{40,16},{48,24},{56,32},{64... | collective-permute-start | bytes 1769480 | tf_op jit(solution)/shard_map/ppermute | solution.py:15
  106.4 13.5 %collective-permute-start.14 = (bf16[2,384,384]{1,2,0:T(8,128)(2,1)}, bf16[2,384,384]{1,2,0:T(8,128)(2,1)S(1)}, u32[]{:S(2)}, u32[]{:S(2)}) collective-permute-start(bf16[2,384,384]{1,2,0:T(8,128)(2,1)} %pad_maximum_fusion), channel_id=1, source_target_pairs={{0,224},{8,232},{16,240},{24,248},{32,0},{40,8},{48,16},{56,24},{6... | collective-permute-start | bytes 1769480 | tf_op jit(solution)/shard_map/ppermute | solution.py:15
  134.1 13.9 %collective-permute-start.21 = (bf16[384,384]{1,0:T(8,128)(2,1)S(1)}, bf16[384,384]{1,0:T(8,128)(2,1)S(1)}, u32[]{:S(2)}, u32[]{:S(2)}) collective-permute-start(bf16[384,384]{1,0:T(8,128)(2,1)S(1)} %convolution_convert_fusion), channel_id=1, source_target_pairs={{0,7},{1,0},{2,1},{3,2},{4,3},{5,4},{6,5},{7,6},{8,15},{9,8},{10,9... | collective-permute-start | bytes 884744 | tf_op jit(solution)/shard_map/ppermute | solution.py:15
  136.0 14.6 %collective-permute-start.20 = (bf16[384,384]{1,0:T(8,128)(2,1)S(1)}, bf16[384,384]{1,0:T(8,128)(2,1)S(1)}, u32[]{:S(2)}, u32[]{:S(2)}) collective-permute-start(bf16[384,384]{1,0:T(8,128)(2,1)S(1)} %convolution_convert_fusion.1), channel_id=1, source_target_pairs={{0,6},{1,7},{2,0},{3,1},{4,2},{5,3},{6,4},{7,5},{8,14},{9,15},{10,... | collective-permute-start | bytes 884744 | tf_op jit(solution)/shard_map/ppermute | solution.py:15
  139.0 19.0 %collective-permute-start.19 = (bf16[384,384]{1,0:T(8,128)(2,1)S(1)}, bf16[384,384]{1,0:T(8,128)(2,1)S(1)}, u32[]{:S(2)}, u32[]{:S(2)}) collective-permute-start(bf16[384,384]{1,0:T(8,128)(2,1)S(1)} %convolution_convert_fusion.2), channel_id=1, source_target_pairs={{0,5},{1,6},{2,7},{3,0},{4,1},{5,2},{6,3},{7,4},{8,13},{9,14},{10,... | collective-permute-start | bytes 884744 | tf_op jit(solution)/shard_map/ppermute | solution.py:15
  141.6 24.5 %collective-permute-start.18 = (bf16[384,384]{1,0:T(8,128)(2,1)S(1)}, bf16[384,384]{1,0:T(8,128)(2,1)S(1)}, u32[]{:S(2)}, u32[]{:S(2)}) collective-permute-start(bf16[384,384]{1,0:T(8,128)(2,1)S(1)} %convolution_convert_fusion.3), channel_id=1, source_target_pairs={{0,4},{1,5},{2,6},{3,7},{4,0},{5,1},{6,2},{7,3},{8,12},{9,13},{10,... | collective-permute-start | bytes 884744 | tf_op jit(solution)/shard_map/ppermute | solution.py:15
  142.6 23.4 %collective-permute-start.17 = (bf16[384,384]{1,0:T(8,128)(2,1)S(1)}, bf16[384,384]{1,0:T(8,128)(2,1)S(1)}, u32[]{:S(2)}, u32[]{:S(2)}) collective-permute-start(bf16[384,384]{1,0:T(8,128)(2,1)S(1)} %convolution_convert_fusion.4), channel_id=1, source_target_pairs={{0,3},{1,4},{2,5},{3,6},{4,7},{5,0},{6,1},{7,2},{8,11},{9,12},{10,... | collective-permute-start | bytes 884744 | tf_op jit(solution)/shard_map/ppermute | solution.py:15
  148.0 18.0 %collective-permute-start.16 = (bf16[384,384]{1,0:T(8,128)(2,1)S(1)}, bf16[384,384]{1,0:T(8,128)(2,1)S(1)}, u32[]{:S(2)}, u32[]{:S(2)}) collective-permute-start(bf16[384,384]{1,0:T(8,128)(2,1)S(1)} %convolution_convert_fusion.5), channel_id=1, source_target_pairs={{0,2},{1,3},{2,4},{3,5},{4,6},{5,7},{6,0},{7,1},{8,10},{9,11},{10,... | collective-permute-start | bytes 884744 | tf_op jit(solution)/shard_map/ppermute | solution.py:15
  150.6 15.5 %collective-permute-start.15 = (bf16[384,384]{1,0:T(8,128)(2,1)S(1)}, bf16[384,384]{1,0:T(8,128)(2,1)S(1)}, u32[]{:S(2)}, u32[]{:S(2)}) collective-permute-start(bf16[384,384]{1,0:T(8,128)(2,1)S(1)} %convolution_convert_fusion.6), channel_id=1, source_target_pairs={{0,1},{1,2},{2,3},{3,4},{4,5},{5,6},{6,7},{7,0},{8,9},{9,10},{10,1... | collective-permute-start | bytes 884744 | tf_op jit(solution)/shard_map/ppermute | solution.py:15
  (6 other events, 25.3 us)

commit v2 on v1

--- a/solution.py
+++ b/solution.py
@@ -27,7 +27,6 @@
     heads_here = columns // HD
     tiles_here = tok_rows // TILE
     total_tiles = neighbours.shape[0]
-    span_here = (REACH + tiles_here - 1) // tiles_here
     flat_w = w_qkv.reshape(w_qkv.shape[0], 3 * columns)
     feats = tokens.shape[1]
     mp_count = lax.axis_size("mp")
@@ -48,25 +47,43 @@
     key_part = head_norm(projected[:, columns : 2 * columns], k_gain).reshape(tok_rows, columns)
     value_part = projected[:, 2 * columns :].astype(jnp.bfloat16)
     paired = jnp.stack([key_part, value_part])
-    blocks = []
-    for offset in range(-span_here, span_here + 1):
-        if offset == 0:
-            blocks.append(paired)
-        else:
-            blocks.append(passed_along(paired, "seq", -offset))
-    window = jnp.concatenate(blocks, axis=1)
-    window_tiles = (2 * span_here + 1) * tiles_here
     position = lax.axis_index("seq")
-    first_tile = position * tiles_here - span_here * tiles_here
-    listed = lax.dynamic_slice_in_dim(neighbours, position * tiles_here, tiles_here, 0)
-    used_counts = lax.dynamic_slice_in_dim(counts, position * tiles_here, tiles_here, 0)
-    relative = jnp.mod(listed - first_tile, total_tiles)
+    seq_count = lax.axis_size("seq")
+    core = position % 2
+    partner = [(source, source ^ 1) for source in range(seq_count)]
+    from_m4 = passed_along(paired, "seq", 4)
+    from_m2 = passed_along(paired, "seq", 2)
+    from_p2 = passed_along(paired, "seq", -2)
+    from_p4 = passed_along(paired, "seq", -4)
+    fwd_own = lax.ppermute(paired, "seq", partner)
+    fwd_a = lax.ppermute(from_m2, "seq", partner)
+    fwd_b = lax.ppermute(from_p2, "seq", partner)
+    fwd_c = lax.ppermute(jnp.where(core == 0, from_p4, from_m4), "seq", partner)
+    window = jnp.concatenate(
+        [paired, from_m4, from_m2, from_p2, from_p4, fwd_own, fwd_a, fwd_b, fwd_c], axis=1
+    )
+    odd = core == 1
+    slot_offsets = jnp.stack(
+        [
+            jnp.int32(0),
+            jnp.int32(-4),
+            jnp.int32(-2),
+            jnp.int32(2),
+            jnp.int32(4),
+            jnp.where(odd, -1, 1).astype(jnp.int32),
+            jnp.where(odd, -3, -1).astype(jnp.int32),
+            jnp.where(odd, 1, 3).astype(jnp.int32),
+            jnp.where(odd, 3, -3).astype(jnp.int32),
+        ]
+    )
+    window_tiles = 9
+    slot_tile = jnp.mod(position + slot_offsets, total_tiles)
+    listed = lax.dynamic_slice_in_dim(neighbours, position, 1, 0)
+    used_counts = lax.dynamic_slice_in_dim(counts, position, 1, 0)
     slot_used = jnp.arange(NB, dtype=jnp.int32)[None, :] < used_counts[:, None]
     query_blocks = queries.reshape(tiles_here, TILE, heads_here, HD)
     factor = HD ** (-0.5)
-    hits = (
-        relative[:, :, None] == jnp.arange(window_tiles, dtype=jnp.int32)[None, None, :]
-    ) & slot_used[:, :, None]
+    hits = (listed[:, :, None] == slot_tile[None, None, :]) & slot_used[:, :, None]
     tile_mask = jnp.any(hits, axis=1)
     key_mask = jnp.repeat(tile_mask, TILE, axis=1)
     near_keys = window[0].reshape(window_tiles * TILE, heads_here, HD)

time: 168 us -> 151 us (0.90)
  starting transfers between devices: 69.4 us -> 43.7 us
  local copies, waits for them, and re-layouts: 21.1 us -> 27.1 us
  other arithmetic: 7.76 us -> 9.97 us
    ppermute x22 -> x18, starting transfers between devices: 69.4 us -> 43.2 us  [passed_along(): return lax.ppermute(value, axis, pairs)]
    unnamed x24 -> x21, local copies, waits for them, and re-layouts: 18.2 us -> 21.4 us
    slice x1, local copies, waits for them, and re-layouts: 0.36 us -> 2.92 us  [on_device(): near_keys = window[0].reshape(window_tiles * TILE, heads_here, HD)]
    select_n x1 -> x2, other arithmetic: 0.19 us -> 2.27 us  [the longest x1 2.26 us: on_device(): fwd_c = lax.ppermute(jnp.where(core == 0, from_p4, from_m4), 'seq', partner)]
    ppermute x22 -> x18, waiting for transfers between devices: 46.8 us -> 47.3 us  [passed_along(): return lax.ppermute(value, axis, pairs)]
  transfers between devices with their start and end apart: 22 -> 22, of which waited for: 9 -> 8; matrix products, arithmetic and copies ran while one was open for 18% -> 24% of each run, Pallas kernels for 0% -> 0%
where the time goes in v2:
time: 151 us; the launch traced here: 150 us
  waiting for transfers between devices  47.3 us (31%)
  starting transfers between devices  43.7 us (29%)
  local copies, waits for them, and re-layouts  27.1 us (18%)
  matrix products  21.8 us (14%)
  other arithmetic  9.97 us (7%)
    ppermute x18, waiting for transfers between devices, passed_along(): return lax.ppermute(value, axis, pairs)  47.3 us
    ppermute x18, starting transfers between devices, passed_along(): return lax.ppermute(value, axis, pairs)  43.2 us
    unnamed x21, local copies, waits for them, and re-layouts  21.4 us
    dot_general x7, matrix products, on_device(): jnp.dot(passed_along(tokens, 'mp', step), lax.dynamic_slice_in_dim(flat_w...  7.5 us
    dot_general x1, matrix products, on_device(): jnp.einsum('thqk,khd->tqhd', probs, near_values, preferred_element_type=j...  4.68 us
    reduce_sum x1, other arithmetic, on_device(): probs = (expo / jnp.sum(expo, axis=-1, keepdims=True)).astype(jnp.bfloat16)  4.28 us
    dot_general x1, matrix products, on_device(): jnp.einsum('tqhd,khd->thqk', query_blocks, near_keys, preferred_element_t...  3.72 us
  transfers between devices with their start and end apart: 22, of which 8 were waited for; matrix products, arithmetic and copies ran while one was open for 24% of the time, Pallas kernels for 0%

profile of v2, /device:TPU:8, one launch (start us, length us, event | category | flops | bytes accessed | tf_op | source)
XLA Modules:
  0.0 150.4 jit_solution(607669318442831348)
XLA Ops:
  0.0 4.5 %collective-permute-start.6 = (bf16[384,384]{1,0:T(8,128)(2,1)}, bf16[384,384]{1,0:T(8,128)(2,1)}, u32[]{:S(2)}, u32[]{:S(2)}) collective-permute-start(bf16[384,384]{1,0:T(8,128)(2,1)} %param.7), channel_id=1, source_target_pairs={{0,7},{1,0},{2,1},{3,2},{4,3},{5,4},{6,5},{7,6},{8,15},{9,8},{10,9... | collective-permute-start | bytes 884744 | tf_op jit(solution)/shard_map/ppermute | solution.py:15
  6.9 2.3 %collective-permute-start.3 = (bf16[384,384]{1,0:T(8,128)(2,1)}, bf16[384,384]{1,0:T(8,128)(2,1)S(1)}, u32[]{:S(2)}, u32[]{:S(2)}) collective-permute-start(bf16[384,384]{1,0:T(8,128)(2,1)} %param.7), channel_id=1, source_target_pairs={{0,4},{1,5},{2,6},{3,7},{4,0},{5,1},{6,2},{7,3},{8,12},{9,13},{10,... | collective-permute-start | bytes 884744 | tf_op jit(solution)/shard_map/ppermute | solution.py:15
  11.9 10.4 %copy.15 = bf16[3072,3,384]{0,2,1:T(8,128)(2,1)} copy(bf16[3072,3,384]{2,0,1:T(8,128)(2,1)} %param.8) | data formatting | bytes 14155776 | tf_op args[1]
  22.3 2.0 %fusion.26 = f32[1152,384]{1,0:T(8,128)S(1)} fusion(bf16[384,384]{1,0:T(8,128)(2,1)S(1)} %copy-done.3, bf16[3072,1152]{0,1:T(8,128)(2,1)} %bitcast.80, s32[]{:T(128)S(6)} %select_n.151), kind=kOutput, calls=%fused_computation.38 | convolution fusion | flops 339738624 | bytes 2949124 | tf_op jit(solution)/shard_map/dot_general | solution.py:34
  24.3 3.8 %collective-permute-done = bf16[384,384]{1,0:T(8,128)(2,1)} collective-permute-done((bf16[384,384]{1,0:T(8,128)(2,1)}, bf16[384,384]{1,0:T(8,128)(2,1)}, u32[]{:S(2)}, u32[]{:S(2)}) %collective-permute-start) | collective-permute-done | bytes 294944 | tf_op jit(solution)/shard_map/ppermute | solution.py:15
  28.1 5.3 %collective-permute-start.2 = (bf16[384,384]{1,0:T(8,128)(2,1)S(1)}, bf16[384,384]{1,0:T(8,128)(2,1)S(1)}, u32[]{:S(2)}, u32[]{:S(2)}) collective-permute-start(bf16[384,384]{1,0:T(8,128)(2,1)S(1)} %copy-done.3), channel_id=1, source_target_pairs={{0,3},{1,4},{2,5},{3,6},{4,7},{5,0},{6,1},{7,2},{8,11},{9,12},{10,... | collective-permute-start | bytes 884744 | tf_op jit(solution)/shard_map/ppermute | solution.py:15
  39.3 5.5 %collective-permute-done.2 = bf16[384,384]{1,0:T(8,128)(2,1)S(1)} collective-permute-done((bf16[384,384]{1,0:T(8,128)(2,1)S(1)}, bf16[384,384]{1,0:T(8,128)(2,1)S(1)}, u32[]{:S(2)}, u32[]{:S(2)}) %collective-permute-start.2) | collective-permute-done | bytes 294944 | tf_op jit(solution)/shard_map/ppermute | solution.py:15
  51.6 2.6 %collective-permute-start.8 = (bf16[2,384,384]{1,2,0:T(8,128)(2,1)}, bf16[2,384,384]{1,2,0:T(8,128)(2,1)}, u32[]{:S(2)}, u32[]{:S(2)}) collective-permute-start(bf16[2,384,384]{1,2,0:T(8,128)(2,1)} %get-tuple-element.11), channel_id=1, source_target_pairs={{0,16},{8,24},{16,32},{24,40},{32,48},{40,56},{48,64},{56,72},{64,... | collective-permute-start | bytes 1769480 | tf_op jit(solution)/shard_map/ppermute | solution.py:15
  54.2 3.2 %collective-permute-start.10 = (bf16[2,384,384]{1,2,0:T(8,128)(2,1)}, bf16[2,384,384]{1,2,0:T(8,128)(2,1)}, u32[]{:S(2)}, u32[]{:S(2)}) collective-permute-start(bf16[2,384,384]{1,2,0:T(8,128)(2,1)} %get-tuple-element.11), channel_id=1, source_target_pairs={{0,224},{8,232},{16,240},{24,248},{32,0},{40,8},{48,16},{56,24},{6... | collective-permute-start | bytes 1769480 | tf_op jit(solution)/shard_map/ppermute | solution.py:15
  59.1 2.1 %collective-permute-start.9 = (bf16[2,384,384]{1,2,0:T(8,128)(2,1)}, bf16[2,384,384]{1,2,0:T(8,128)(2,1)}, u32[]{:S(2)}, u32[]{:S(2)}) collective-permute-start(bf16[2,384,384]{1,2,0:T(8,128)(2,1)} %get-tuple-element.11), channel_id=1, source_target_pairs={{0,240},{8,248},{16,0},{24,8},{32,16},{40,24},{48,32},{56,40},{64,... | collective-permute-start | bytes 1769480 | tf_op jit(solution)/shard_map/ppermute | solution.py:15
  61.5 6.8 %collective-permute-done.8 = bf16[2,384,384]{1,2,0:T(8,128)(2,1)} collective-permute-done((bf16[2,384,384]{1,2,0:T(8,128)(2,1)}, bf16[2,384,384]{1,2,0:T(8,128)(2,1)}, u32[]{:S(2)}, u32[]{:S(2)}) %collective-permute-start.8) | collective-permute-done | bytes 589856 | tf_op jit(solution)/shard_map/ppermute | solution.py:15
  68.3 13.2 %collective-permute-done.7 = bf16[2,384,384]{1,2,0:T(8,128)(2,1)} collective-permute-done((bf16[2,384,384]{1,2,0:T(8,128)(2,1)}, bf16[2,384,384]{1,2,0:T(8,128)(2,1)}, u32[]{:S(2)}, u32[]{:S(2)}) %collective-permute-start.7) | collective-permute-done | bytes 589856 | tf_op jit(solution)/shard_map/ppermute | solution.py:15
  81.5 2.3 %broadcast_select_fusion = (bf16[2,384,384]{1,2,0:T(8,128)(2,1)S(1)}, bf16[2,3456,384]{1,2,0:T(8,128)(2,1)}) fusion(bf16[2,384,384]{1,2,0:T(8,128)(2,1)} %collective-permute-done.10, bf16[2,384,384]{1,2,0:T(8,128)(2,1)} %collective-permute-done.7, pred[]{:T(512)S(6)} %eq.45, bf16[2,3456,384]{1,2,0:T(8,128)(2,1)} %get-tuple-element.12), kind=kLoop, calls=%fused_computation.48 | loop fusion | flops 294912 | bytes 2359297 | tf_op jit(solution)/shard_map/jit(_where)/select_n | solution.py:61
  95.0 2.9 %fusion.64 = (bf16[1,3456,384]{1,2,0:T(8,128)(2,1)S(1)}, bf16[1,3456,384]{1,2,0:T(8,128)(2,1)S(1)}) fusion(bf16[2,3456,384]{1,2,0:T(8,128)(2,1)} %constant_dynamic-update-slice_fusion), kind=kLoop, calls=%fused_computation.100 | loop fusion | bytes 10616832 | tf_op jit(solution)/shard_map/slice | solution.py:89
  98.0 3.7 %bitcast_reduce_fusion = (f32[3,384]{1,0:T(4,128)S(1)}, f32[3,3456,384]{2,1,0:T(8,128)S(1)}) fusion(pred[3456]{0:T(1024)(128)(4,1)S(1)} %broadcast_in_dim.13, bf16[3456,3,128]{0,2,1:T(8,128)(2,1)S(1)} %bitcast.96, f32[384,3,128]{2,0,1:T(8,128)S(1)} %copy.16, f32[128]{0:T(128)S(1)} %copy-done.4, f32[384,3]{0,1:T(4,128)S(1)} %add_rsqrt_fusion), kind=kOutput, calls=%fused_computation.1 | convolution fusion | flops 1031601024 | bytes 19182464 | tf_op jit(solution)/shard_map/tqhd,khd->thqk/dot_general | solution.py:92
  101.7 4.3 %fusion.1 = f32[3,384]{1,0:T(4,128)S(1)} fusion(f32[3,3456,384]{2,1,0:T(8,128)S(1)} %get-tuple-element.14, f32[3,384]{1,0:T(4,128)S(1)} %get-tuple-element.13, pred[3456]{0:T(1024)(128)(4,1)S(1)} %broadcast_in_dim.13), kind=kLoop, calls=%fused_computation.5 | loop fusion | flops 15924096 | bytes 15937920 | tf_op jit(solution)/shard_map/reduce_sum | solution.py:98
  106.0 4.7 %fusion.11 = bf16[3,128,384]{2,1,0:T(8,128)(2,1)S(1)} fusion(bf16[3456,3,128]{0,2,1:T(8,128)(2,1)S(1)} %bitcast.99, f32[3,384]{1,0:T(4,128)S(1)} %fusion.1, f32[3,384]{1,0:T(4,128)S(1)} %get-tuple-element.13, f32[3,3456,384]{2,1,0:T(8,128)S(1)} %get-tuple-element.14, pred[3456]{0:T(1024)(128)(4,1)S(1)} %broadcast_in_dim.13), kind=kOutput, calls=%fused_computation.25 | convolution fusion | flops 1039269888 | bytes 18887040 | tf_op jit(solution)/shard_map/thqk,khd->tqhd/dot_general | solution.py:99
  111.0 3.5 %collective-permute-start.21 = (bf16[384,384]{1,0:T(8,128)(2,1)S(1)}, bf16[384,384]{1,0:T(8,128)(2,1)S(1)}, u32[]{:S(2)}, u32[]{:S(2)}) collective-permute-start(bf16[384,384]{1,0:T(8,128)(2,1)S(1)} %convolution_convert_fusion), channel_id=1, source_target_pairs={{0,7},{1,0},{2,1},{3,2},{4,3},{5,4},{6,5},{7,6},{8,15},{9,8},{10,9... | collective-permute-start | bytes 884744 | tf_op jit(solution)/shard_map/ppermute | solution.py:15
  114.9 2.0 %collective-permute-start.20 = (bf16[384,384]{1,0:T(8,128)(2,1)S(1)}, bf16[384,384]{1,0:T(8,128)(2,1)S(1)}, u32[]{:S(2)}, u32[]{:S(2)}) collective-permute-start(bf16[384,384]{1,0:T(8,128)(2,1)S(1)} %convolution_convert_fusion.1), channel_id=1, source_target_pairs={{0,6},{1,7},{2,0},{3,1},{4,2},{5,3},{6,4},{7,5},{8,14},{9,15},{10,... | collective-permute-start | bytes 884744 | tf_op jit(solution)/shard_map/ppermute | solution.py:15
  120.5 3.3 %collective-permute-start.17 = (bf16[384,384]{1,0:T(8,128)(2,1)S(1)}, bf16[384,384]{1,0:T(8,128)(2,1)S(1)}, u32[]{:S(2)}, u32[]{:S(2)}) collective-permute-start(bf16[384,384]{1,0:T(8,128)(2,1)S(1)} %convolution_convert_fusion.4), channel_id=1, source_target_pairs={{0,3},{1,4},{2,5},{3,6},{4,7},{5,0},{6,1},{7,2},{8,11},{9,12},{10,... | collective-permute-start | bytes 884744 | tf_op jit(solution)/shard_map/ppermute | solution.py:15
  124.6 5.4 %collective-permute-done.21 = bf16[384,384]{1,0:T(8,128)(2,1)S(1)} collective-permute-done((bf16[384,384]{1,0:T(8,128)(2,1)S(1)}, bf16[384,384]{1,0:T(8,128)(2,1)S(1)}, u32[]{:S(2)}, u32[]{:S(2)}) %collective-permute-start.21) | collective-permute-done | bytes 294944 | tf_op jit(solution)/shard_map/ppermute | solution.py:15
  130.0 7.6 %collective-permute-start.15 = (bf16[384,384]{1,0:T(8,128)(2,1)S(1)}, bf16[384,384]{1,0:T(8,128)(2,1)S(1)}, u32[]{:S(2)}, u32[]{:S(2)}) collective-permute-start(bf16[384,384]{1,0:T(8,128)(2,1)S(1)} %convolution_convert_fusion.6), channel_id=1, source_target_pairs={{0,1},{1,2},{2,3},{3,4},{4,5},{5,6},{6,7},{7,0},{8,9},{9,10},{10,1... | collective-permute-start | bytes 884744 | tf_op jit(solution)/shard_map/ppermute | solution.py:15
  137.6 8.5 %collective-permute-done.16 = bf16[384,384]{1,0:T(8,128)(2,1)S(1)} collective-permute-done((bf16[384,384]{1,0:T(8,128)(2,1)S(1)}, bf16[384,384]{1,0:T(8,128)(2,1)S(1)}, u32[]{:S(2)}, u32[]{:S(2)}) %collective-permute-start.16) | collective-permute-done | bytes 294944 | tf_op jit(solution)/shard_map/ppermute | solution.py:15
  146.1 3.0 %collective-permute-done.15 = bf16[384,384]{1,0:T(8,128)(2,1)S(1)} collective-permute-done((bf16[384,384]{1,0:T(8,128)(2,1)S(1)}, bf16[384,384]{1,0:T(8,128)(2,1)S(1)}, u32[]{:S(2)}, u32[]{:S(2)}) %collective-permute-start.15) | collective-permute-done | bytes 294944 | tf_op jit(solution)/shard_map/ppermute | solution.py:15
  (81 shorter events, 37.1 us)
Async XLA Ops:
  0.0 110.7 %copy-start = (bf16[384,3072]{1,0:T(8,128)(2,1)S(1)}, bf16[384,3072]{1,0:T(8,128)(2,1)}, u32[]{:S(2)}) copy-start(bf16[384,3072]{1,0:T(8,128)(2,1)} %param.11) | copy-start | bytes 7077892
  0.0 35.3 %collective-permute-start.6 = (bf16[384,384]{1,0:T(8,128)(2,1)}, bf16[384,384]{1,0:T(8,128)(2,1)}, u32[]{:S(2)}, u32[]{:S(2)}) collective-permute-start(bf16[384,384]{1,0:T(8,128)(2,1)} %param.7), channel_id=1, source_target_pairs={{0,7},{1,0},{2,1},{3,2},{4,3},{5,4},{6,5},{7,6},{8,15},{9,8},{10,9... | collective-permute-start | bytes 884744 | tf_op jit(solution)/shard_map/ppermute | solution.py:15
  4.5 32.6 %collective-permute-start.5 = (bf16[384,384]{1,0:T(8,128)(2,1)}, bf16[384,384]{1,0:T(8,128)(2,1)S(1)}, u32[]{:S(2)}, u32[]{:S(2)}) collective-permute-start(bf16[384,384]{1,0:T(8,128)(2,1)} %param.7), channel_id=1, source_target_pairs={{0,6},{1,7},{2,0},{3,1},{4,2},{5,3},{6,4},{7,5},{8,14},{9,15},{10,... | collective-permute-start | bytes 884744 | tf_op jit(solution)/shard_map/ppermute | solution.py:15
  5.3 32.6 %collective-permute-start.4 = (bf16[384,384]{1,0:T(8,128)(2,1)}, bf16[384,384]{1,0:T(8,128)(2,1)S(1)}, u32[]{:S(2)}, u32[]{:S(2)}) collective-permute-start(bf16[384,384]{1,0:T(8,128)(2,1)} %param.7), channel_id=1, source_target_pairs={{0,5},{1,6},{2,7},{3,0},{4,1},{5,2},{6,3},{7,4},{8,13},{9,14},{10,... | collective-permute-start | bytes 884744 | tf_op jit(solution)/shard_map/ppermute | solution.py:15
  6.9 31.7 %collective-permute-start.3 = (bf16[384,384]{1,0:T(8,128)(2,1)}, bf16[384,384]{1,0:T(8,128)(2,1)S(1)}, u32[]{:S(2)}, u32[]{:S(2)}) collective-permute-start(bf16[384,384]{1,0:T(8,128)(2,1)} %param.7), channel_id=1, source_target_pairs={{0,4},{1,5},{2,6},{3,7},{4,0},{5,1},{6,2},{7,3},{8,12},{9,13},{10,... | collective-permute-start | bytes 884744 | tf_op jit(solution)/shard_map/ppermute | solution.py:15
  9.1 18.9 %collective-permute-start = (bf16[384,384]{1,0:T(8,128)(2,1)}, bf16[384,384]{1,0:T(8,128)(2,1)}, u32[]{:S(2)}, u32[]{:S(2)}) collective-permute-start(bf16[384,384]{1,0:T(8,128)(2,1)} %param.7), channel_id=1, source_target_pairs={{0,1},{1,2},{2,3},{3,4},{4,5},{5,6},{6,7},{7,0},{8,9},{9,10},{10,1... | collective-permute-start | bytes 884744 | tf_op jit(solution)/shard_map/ppermute | solution.py:15
  22.3 13.2 %copy-start.1 = (bf16[3072,3,384]{0,2,1:T(8,128)(2,1)S(1)}, bf16[3072,3,384]{0,2,1:T(8,128)(2,1)}, u32[]{:S(2)}) copy-start(bf16[3072,3,384]{0,2,1:T(8,128)(2,1)} %copy.15) | copy-start | bytes 21233668
  28.1 16.8 %collective-permute-start.2 = (bf16[384,384]{1,0:T(8,128)(2,1)S(1)}, bf16[384,384]{1,0:T(8,128)(2,1)S(1)}, u32[]{:S(2)}, u32[]{:S(2)}) collective-permute-start(bf16[384,384]{1,0:T(8,128)(2,1)S(1)} %copy-done.3), channel_id=1, source_target_pairs={{0,3},{1,4},{2,5},{3,6},{4,7},{5,0},{6,1},{7,2},{8,11},{9,12},{10,... | collective-permute-start | bytes 884744 | tf_op jit(solution)/shard_map/ppermute | solution.py:15
  35.3 11.3 %collective-permute-start.1 = (bf16[384,384]{1,0:T(8,128)(2,1)S(1)}, bf16[384,384]{1,0:T(8,128)(2,1)S(1)}, u32[]{:S(2)}, u32[]{:S(2)}) collective-permute-start(bf16[384,384]{1,0:T(8,128)(2,1)S(1)} %copy-done.3), channel_id=1, source_target_pairs={{0,2},{1,3},{2,4},{3,5},{4,6},{5,7},{6,0},{7,1},{8,10},{9,11},{10,... | collective-permute-start | bytes 884744 | tf_op jit(solution)/shard_map/ppermute | solution.py:15
  51.6 16.7 %collective-permute-start.8 = (bf16[2,384,384]{1,2,0:T(8,128)(2,1)}, bf16[2,384,384]{1,2,0:T(8,128)(2,1)}, u32[]{:S(2)}, u32[]{:S(2)}) collective-permute-start(bf16[2,384,384]{1,2,0:T(8,128)(2,1)} %get-tuple-element.11), channel_id=1, source_target_pairs={{0,16},{8,24},{16,32},{24,40},{32,48},{40,56},{48,64},{56,72},{64,... | collective-permute-start | bytes 1769480 | tf_op jit(solution)/shard_map/ppermute | solution.py:15
  54.2 14.1 %collective-permute-start.10 = (bf16[2,384,384]{1,2,0:T(8,128)(2,1)}, bf16[2,384,384]{1,2,0:T(8,128)(2,1)}, u32[]{:S(2)}, u32[]{:S(2)}) collective-permute-start(bf16[2,384,384]{1,2,0:T(8,128)(2,1)} %get-tuple-element.11), channel_id=1, source_target_pairs={{0,224},{8,232},{16,240},{24,248},{32,0},{40,8},{48,16},{56,24},{6... | collective-permute-start | bytes 1769480 | tf_op jit(solution)/shard_map/ppermute | solution.py:15
  57.4 24.0 %collective-permute-start.7 = (bf16[2,384,384]{1,2,0:T(8,128)(2,1)}, bf16[2,384,384]{1,2,0:T(8,128)(2,1)}, u32[]{:S(2)}, u32[]{:S(2)}) collective-permute-start(bf16[2,384,384]{1,2,0:T(8,128)(2,1)} %get-tuple-element.11), channel_id=1, source_target_pairs={{0,32},{8,40},{16,48},{24,56},{32,64},{40,72},{48,80},{56,88},{64,... | collective-permute-start | bytes 1769480 | tf_op jit(solution)/shard_map/ppermute | solution.py:15
  59.1 24.6 %collective-permute-start.9 = (bf16[2,384,384]{1,2,0:T(8,128)(2,1)}, bf16[2,384,384]{1,2,0:T(8,128)(2,1)}, u32[]{:S(2)}, u32[]{:S(2)}) collective-permute-start(bf16[2,384,384]{1,2,0:T(8,128)(2,1)} %get-tuple-element.11), channel_id=1, source_target_pairs={{0,240},{8,248},{16,0},{24,8},{32,16},{40,24},{48,32},{56,40},{64,... | collective-permute-start | bytes 1769480 | tf_op jit(solution)/shard_map/ppermute | solution.py:15
  61.2 29.0 %collective-permute-start.11 = (bf16[2,384,384]{1,2,0:T(8,128)(2,1)}, bf16[2,384,384]{1,2,0:T(8,128)(2,1)}, u32[]{:S(2)}, u32[]{:S(2)}) collective-permute-start(bf16[2,384,384]{1,2,0:T(8,128)(2,1)} %get-tuple-element.11), channel_id=1, source_target_pairs={{0,8},{8,0},{16,24},{24,16},{32,40},{40,32},{48,56},{56,48},{64,72... | collective-permute-start | bytes 1769480 | tf_op jit(solution)/shard_map/ppermute | solution.py:58
  68.3 23.9 %collective-permute-start.12 = (bf16[2,384,384]{1,2,0:T(8,128)(2,1)}, bf16[2,384,384]{1,2,0:T(8,128)(2,1)S(1)}, u32[]{:S(2)}, u32[]{:S(2)}) collective-permute-start(bf16[2,384,384]{1,2,0:T(8,128)(2,1)} %collective-permute-done.8), channel_id=1, source_target_pairs={{0,8},{8,0},{16,24},{24,16},{32,40},{40,32},{48,56},{56,48},{64,72... | collective-permute-start | bytes 1769480 | tf_op jit(solution)/shard_map/ppermute | solution.py:59
  83.7 10.4 %collective-permute-start.14 = (bf16[2,384,384]{1,2,0:T(8,128)(2,1)S(1)}, bf16[2,384,384]{1,2,0:T(8,128)(2,1)S(1)}, u32[]{:S(2)}, u32[]{:S(2)}) collective-permute-start(bf16[2,384,384]{1,2,0:T(8,128)(2,1)S(1)} %get-tuple-element.9), channel_id=1, source_target_pairs={{0,8},{8,0},{16,24},{24,16},{32,40},{40,32},{48,56},{56,48},{64,72... | collective-permute-start | bytes 1769480 | tf_op jit(solution)/shard_map/ppermute | solution.py:61
  83.7 9.4 %collective-permute-start.13 = (bf16[2,384,384]{1,2,0:T(8,128)(2,1)}, bf16[2,384,384]{1,2,0:T(8,128)(2,1)S(1)}, u32[]{:S(2)}, u32[]{:S(2)}) collective-permute-start(bf16[2,384,384]{1,2,0:T(8,128)(2,1)} %collective-permute-done.9), channel_id=1, source_target_pairs={{0,8},{8,0},{16,24},{24,16},{32,40},{40,32},{48,56},{56,48},{64,72... | collective-permute-start | bytes 1769480 | tf_op jit(solution)/shard_map/ppermute | solution.py:60
  111.0 19.0 %collective-permute-start.21 = (bf16[384,384]{1,0:T(8,128)(2,1)S(1)}, bf16[384,384]{1,0:T(8,128)(2,1)S(1)}, u32[]{:S(2)}, u32[]{:S(2)}) collective-permute-start(bf16[384,384]{1,0:T(8,128)(2,1)S(1)} %convolution_convert_fusion), channel_id=1, source_target_pairs={{0,7},{1,0},{2,1},{3,2},{4,3},{5,4},{6,5},{7,6},{8,15},{9,8},{10,9... | collective-permute-start | bytes 884744 | tf_op jit(solution)/shard_map/ppermute | solution.py:15
  114.9 15.1 %collective-permute-start.20 = (bf16[384,384]{1,0:T(8,128)(2,1)S(1)}, bf16[384,384]{1,0:T(8,128)(2,1)S(1)}, u32[]{:S(2)}, u32[]{:S(2)}) collective-permute-start(bf16[384,384]{1,0:T(8,128)(2,1)S(1)} %convolution_convert_fusion.1), channel_id=1, source_target_pairs={{0,6},{1,7},{2,0},{3,1},{4,2},{5,3},{6,4},{7,5},{8,14},{9,15},{10,... | collective-permute-start | bytes 884744 | tf_op jit(solution)/shard_map/ppermute | solution.py:15
  117.3 20.3 %collective-permute-start.19 = (bf16[384,384]{1,0:T(8,128)(2,1)S(1)}, bf16[384,384]{1,0:T(8,128)(2,1)S(1)}, u32[]{:S(2)}, u32[]{:S(2)}) collective-permute-start(bf16[384,384]{1,0:T(8,128)(2,1)S(1)} %convolution_convert_fusion.2), channel_id=1, source_target_pairs={{0,5},{1,6},{2,7},{3,0},{4,1},{5,2},{6,3},{7,4},{8,13},{9,14},{10,... | collective-permute-start | bytes 884744 | tf_op jit(solution)/shard_map/ppermute | solution.py:15
  118.7 19.0 %collective-permute-start.18 = (bf16[384,384]{1,0:T(8,128)(2,1)S(1)}, bf16[384,384]{1,0:T(8,128)(2,1)S(1)}, u32[]{:S(2)}, u32[]{:S(2)}) collective-permute-start(bf16[384,384]{1,0:T(8,128)(2,1)S(1)} %convolution_convert_fusion.3), channel_id=1, source_target_pairs={{0,4},{1,5},{2,6},{3,7},{4,0},{5,1},{6,2},{7,3},{8,12},{9,13},{10,... | collective-permute-start | bytes 884744 | tf_op jit(solution)/shard_map/ppermute | solution.py:15
  120.5 17.1 %collective-permute-start.17 = (bf16[384,384]{1,0:T(8,128)(2,1)S(1)}, bf16[384,384]{1,0:T(8,128)(2,1)S(1)}, u32[]{:S(2)}, u32[]{:S(2)}) collective-permute-start(bf16[384,384]{1,0:T(8,128)(2,1)S(1)} %convolution_convert_fusion.4), channel_id=1, source_target_pairs={{0,3},{1,4},{2,5},{3,6},{4,7},{5,0},{6,1},{7,2},{8,11},{9,12},{10,... | collective-permute-start | bytes 884744 | tf_op jit(solution)/shard_map/ppermute | solution.py:15
  130.0 16.1 %collective-permute-start.16 = (bf16[384,384]{1,0:T(8,128)(2,1)S(1)}, bf16[384,384]{1,0:T(8,128)(2,1)S(1)}, u32[]{:S(2)}, u32[]{:S(2)}) collective-permute-start(bf16[384,384]{1,0:T(8,128)(2,1)S(1)} %convolution_convert_fusion.5), channel_id=1, source_target_pairs={{0,2},{1,3},{2,4},{3,5},{4,6},{5,7},{6,0},{7,1},{8,10},{9,11},{10,... | collective-permute-start | bytes 884744 | tf_op jit(solution)/shard_map/ppermute | solution.py:15
  130.0 19.1 %collective-permute-start.15 = (bf16[384,384]{1,0:T(8,128)(2,1)S(1)}, bf16[384,384]{1,0:T(8,128)(2,1)S(1)}, u32[]{:S(2)}, u32[]{:S(2)}) collective-permute-start(bf16[384,384]{1,0:T(8,128)(2,1)S(1)} %convolution_convert_fusion.6), channel_id=1, source_target_pairs={{0,1},{1,2},{2,3},{3,4},{4,5},{5,6},{6,7},{7,0},{8,9},{9,10},{10,1... | collective-permute-start | bytes 884744 | tf_op jit(solution)/shard_map/ppermute | solution.py:15
  (5 other events, 34.1 us)

commit v3 on v2

--- a/solution.py
+++ b/solution.py
@@ -27,25 +27,27 @@
     heads_here = columns // HD
     tiles_here = tok_rows // TILE
     total_tiles = neighbours.shape[0]
-    flat_w = w_qkv.reshape(w_qkv.shape[0], 3 * columns)
     feats = tokens.shape[1]
     mp_count = lax.axis_size("mp")
     mp_here = lax.axis_index("mp")
-    projected = jnp.dot(
-        tokens,
-        lax.dynamic_slice_in_dim(flat_w, mp_here * feats, feats, 0),
-        preferred_element_type=jnp.float32,
+
+    def rows_of(block):
+        return lax.dynamic_slice_in_dim(w_qkv, block * feats, feats, 0)
+
+    projected = jnp.einsum(
+        "tf,fjc->jtc", tokens, rows_of(mp_here), preferred_element_type=jnp.float32
     )
     for step in range(1, mp_count):
         source = (mp_here - step) % mp_count
-        projected = projected + jnp.dot(
+        projected = projected + jnp.einsum(
+            "tf,fjc->jtc",
             passed_along(tokens, "mp", step),
-            lax.dynamic_slice_in_dim(flat_w, source * feats, feats, 0),
+            rows_of(source),
             preferred_element_type=jnp.float32,
         )
-    queries = head_norm(projected[:, :columns], q_gain)
-    key_part = head_norm(projected[:, columns : 2 * columns], k_gain).reshape(tok_rows, columns)
-    value_part = projected[:, 2 * columns :].astype(jnp.bfloat16)
+    queries = head_norm(projected[0], q_gain)
+    key_part = head_norm(projected[1], k_gain).reshape(tok_rows, columns)
+    value_part = projected[2].astype(jnp.bfloat16)
     paired = jnp.stack([key_part, value_part])
     position = lax.axis_index("seq")
     seq_count = lax.axis_size("seq")

time: 151 us -> 144 us (0.954)
  local copies, waits for them, and re-layouts: 27.1 us -> 16.8 us
  starting transfers between devices: 43.7 us -> 37 us
  waiting for transfers between devices: 47.3 us -> 53.4 us
  matrix products: 21.8 us -> 25.2 us
    unnamed x21 -> x22, local copies, waits for them, and re-layouts: 21.4 us -> 11 us
    ppermute x18, starting transfers between devices: 43.2 us -> 36.5 us  [passed_along(): return lax.ppermute(value, axis, pairs)]
    ppermute x18, waiting for transfers between devices: 47.3 us -> 53.4 us  [passed_along(): return lax.ppermute(value, axis, pairs)]
    dot_general x8, matrix products: 9.52 us -> 12.9 us  [the longest x7 9.66 us: on_device(): jnp.einsum('tf,fjc->jtc', passed_along(tokens, 'mp', step), rows_of(sourc...]
  transfers between devices with their start and end apart: 22 -> 22, of which waited for: 8 -> 9; matrix products, arithmetic and copies ran while one was open for 24% -> 20% of each run, Pallas kernels for 0% -> 0%
where the time goes in v3:
time: 144 us; the launch traced here: 143 us
  waiting for transfers between devices  53.4 us (37%)
  starting transfers between devices  37 us (26%)
  matrix products  25.2 us (18%)
  local copies, waits for them, and re-layouts  16.8 us (12%)
  other arithmetic  10 us (7%)
    ppermute x18, waiting for transfers between devices, passed_along(): return lax.ppermute(value, axis, pairs)  53.4 us
    ppermute x18, starting transfers between devices, passed_along(): return lax.ppermute(value, axis, pairs)  36.5 us
    unnamed x22, local copies, waits for them, and re-layouts  11 us
    dot_general x7, matrix products, on_device(): jnp.einsum('tf,fjc->jtc', passed_along(tokens, 'mp', step), rows_of(sourc...  9.66 us
    dot_general x1, matrix products, on_device(): jnp.einsum('thqk,khd->tqhd', probs, near_values, preferred_element_type=j...  4.68 us
    reduce_sum x1, other arithmetic, on_device(): probs = (expo / jnp.sum(expo, axis=-1, keepdims=True)).astype(jnp.bfloat16)  4.28 us
    dot_general x1, matrix products, on_device(): jnp.einsum('tqhd,khd->thqk', query_blocks, near_keys, preferred_element_t...  3.72 us
    dot_general x1, matrix products, on_device(): jnp.einsum('tf,fjc->jtc', tokens, rows_of(mp_here), preferred_element_typ...  3.21 us
  transfers between devices with their start and end apart: 22, of which 9 were waited for; matrix products, arithmetic and copies ran while one was open for 20% of the time, Pallas kernels for 0%

profile of v3, /device:TPU:8, one launch (start us, length us, event | category | flops | bytes accessed | tf_op | source)
XLA Modules:
  0.0 143.1 jit_solution(2647722839122191338)
XLA Ops:
  0.0 4.8 %collective-permute-start.5 = (bf16[384,384]{1,0:T(8,128)(2,1)}, bf16[384,384]{1,0:T(8,128)(2,1)}, u32[]{:S(2)}, u32[]{:S(2)}) collective-permute-start(bf16[384,384]{1,0:T(8,128)(2,1)} %param.7), channel_id=1, source_target_pairs={{0,6},{1,7},{2,0},{3,1},{4,2},{5,3},{6,4},{7,5},{8,14},{9,15},{10,... | collective-permute-start | bytes 884744 | tf_op jit(solution)/shard_map/ppermute | solution.py:15
  6.0 2.3 %collective-permute-start.3 = (bf16[384,384]{1,0:T(8,128)(2,1)}, bf16[384,384]{1,0:T(8,128)(2,1)S(1)}, u32[]{:S(2)}, u32[]{:S(2)}) collective-permute-start(bf16[384,384]{1,0:T(8,128)(2,1)} %param.7), channel_id=1, source_target_pairs={{0,4},{1,5},{2,6},{3,7},{4,0},{5,1},{6,2},{7,3},{8,12},{9,13},{10,... | collective-permute-start | bytes 884744 | tf_op jit(solution)/shard_map/ppermute | solution.py:15
  10.4 3.2 %fusion.24 = f32[3,384,384]{2,1,0:T(8,128)} fusion(bf16[3072,3,384]{2,0,1:T(8,128)(2,1)} %param.8, s32[]{:T(128)S(6)} %select_n.151, bf16[384,384]{1,0:T(8,128)(2,1)} %param.7), kind=kOutput, calls=%fused_computation.33 | convolution fusion | flops 339738624 | bytes 2949124 | tf_op jit(solution)/shard_map/tf,fjc->jtc/dot_general | solution.py:37
  16.0 2.5 %fusion.12 = f32[3,384,384]{2,1,0:T(8,128)S(1)} fusion(bf16[3072,3,384]{2,0,1:T(8,128)(2,1)} %param.8, s32[]{:T(128)S(6)} %select_n.163, bf16[384,384]{1,0:T(8,128)(2,1)} %collective-permute-done.5), kind=kOutput, calls=%fused_computation.21 | convolution fusion | flops 339738624 | bytes 2949124 | tf_op jit(solution)/shard_map/tf,fjc->jtc/dot_general | solution.py:42
  18.5 4.3 %collective-permute-done.4 = bf16[384,384]{1,0:T(8,128)(2,1)} collective-permute-done((bf16[384,384]{1,0:T(8,128)(2,1)}, bf16[384,384]{1,0:T(8,128)(2,1)}, u32[]{:S(2)}, u32[]{:S(2)}) %collective-permute-start.4) | collective-permute-done | bytes 294944 | tf_op jit(solution)/shard_map/ppermute | solution.py:15
  22.9 2.1 %collective-permute-start.6 = (bf16[384,384]{1,0:T(8,128)(2,1)S(1)}, bf16[384,384]{1,0:T(8,128)(2,1)S(1)}, u32[]{:S(2)}, u32[]{:S(2)}) collective-permute-start(bf16[384,384]{1,0:T(8,128)(2,1)S(1)} %copy-done.4), channel_id=1, source_target_pairs={{0,7},{1,0},{2,1},{3,2},{4,3},{5,4},{6,5},{7,6},{8,15},{9,8},{10,9... | collective-permute-start | bytes 884744 | tf_op jit(solution)/shard_map/ppermute | solution.py:15
  26.9 7.9 %collective-permute-done.3 = bf16[384,384]{1,0:T(8,128)(2,1)S(1)} collective-permute-done((bf16[384,384]{1,0:T(8,128)(2,1)}, bf16[384,384]{1,0:T(8,128)(2,1)S(1)}, u32[]{:S(2)}, u32[]{:S(2)}) %collective-permute-start.3) | collective-permute-done | bytes 294944 | tf_op jit(solution)/shard_map/ppermute | solution.py:15
  45.9 4.0 %collective-permute-start.10 = (bf16[2,384,384]{1,2,0:T(8,128)(2,1)}, bf16[2,384,384]{1,2,0:T(8,128)(2,1)}, u32[]{:S(2)}, u32[]{:S(2)}) collective-permute-start(bf16[2,384,384]{1,2,0:T(8,128)(2,1)} %get-tuple-element.11), channel_id=1, source_target_pairs={{0,224},{8,232},{16,240},{24,248},{32,0},{40,8},{48,16},{56,24},{6... | collective-permute-start | bytes 1769480 | tf_op jit(solution)/shard_map/ppermute | solution.py:15
  51.6 2.1 %collective-permute-start.9 = (bf16[2,384,384]{1,2,0:T(8,128)(2,1)}, bf16[2,384,384]{1,2,0:T(8,128)(2,1)}, u32[]{:S(2)}, u32[]{:S(2)}) collective-permute-start(bf16[2,384,384]{1,2,0:T(8,128)(2,1)} %get-tuple-element.11), channel_id=1, source_target_pairs={{0,240},{8,248},{16,0},{24,8},{32,16},{40,24},{48,32},{56,40},{64,... | collective-permute-start | bytes 1769480 | tf_op jit(solution)/shard_map/ppermute | solution.py:15
  54.0 6.0 %collective-permute-done.8 = bf16[2,384,384]{1,2,0:T(8,128)(2,1)} collective-permute-done((bf16[2,384,384]{1,2,0:T(8,128)(2,1)}, bf16[2,384,384]{1,2,0:T(8,128)(2,1)}, u32[]{:S(2)}, u32[]{:S(2)}) %collective-permute-start.8) | collective-permute-done | bytes 589856 | tf_op jit(solution)/shard_map/ppermute | solution.py:15
  61.4 13.4 %collective-permute-done.7 = bf16[2,384,384]{1,2,0:T(8,128)(2,1)} collective-permute-done((bf16[2,384,384]{1,2,0:T(8,128)(2,1)}, bf16[2,384,384]{1,2,0:T(8,128)(2,1)}, u32[]{:S(2)}, u32[]{:S(2)}) %collective-permute-start.7) | collective-permute-done | bytes 589856 | tf_op jit(solution)/shard_map/ppermute | solution.py:15
  74.8 2.3 %broadcast_select_fusion = (bf16[2,384,384]{1,2,0:T(8,128)(2,1)S(1)}, bf16[2,3456,384]{1,2,0:T(8,128)(2,1)}) fusion(bf16[2,384,384]{1,2,0:T(8,128)(2,1)} %collective-permute-done.10, bf16[2,384,384]{1,2,0:T(8,128)(2,1)} %collective-permute-done.7, pred[]{:T(512)S(6)} %eq.45, bf16[2,3456,384]{1,2,0:T(8,128)(2,1)} %get-tuple-element.12), kind=kLoop, calls=%fused_computation.43 | loop fusion | flops 294912 | bytes 2359297 | tf_op jit(solution)/shard_map/jit(_where)/select_n | solution.py:63
  88.5 2.9 %fusion.69 = (bf16[1,3456,384]{1,2,0:T(8,128)(2,1)S(1)}, bf16[1,3456,384]{1,2,0:T(8,128)(2,1)S(1)}) fusion(bf16[2,3456,384]{1,2,0:T(8,128)(2,1)} %constant_dynamic-update-slice_fusion), kind=kLoop, calls=%fused_computation.102 | loop fusion | bytes 10616832 | tf_op jit(solution)/shard_map/slice | solution.py:91
  91.4 3.7 %bitcast_reduce_fusion = (f32[3,384]{1,0:T(4,128)S(1)}, f32[3,3456,384]{2,1,0:T(8,128)S(1)}) fusion(pred[3456]{0:T(1024)(128)(4,1)S(1)} %broadcast_in_dim.13, bf16[3456,3,128]{0,2,1:T(8,128)(2,1)S(1)} %bitcast.100, f32[384,3,128]{2,0,1:T(8,128)S(1)} %copy.27, f32[128]{0:T(128)S(1)} %copy-done.5, f32[384,3]{0,1:T(4,128)S(1)} %add_rsqrt_fusion), kind=kOutput, calls=%fused_computation.1 | convolution fusion | flops 1031601024 | bytes 19182464 | tf_op jit(solution)/shard_map/tqhd,khd->thqk/dot_general | solution.py:94
  95.1 4.3 %fusion.1 = f32[3,384]{1,0:T(4,128)S(1)} fusion(f32[3,3456,384]{2,1,0:T(8,128)S(1)} %get-tuple-element.14, f32[3,384]{1,0:T(4,128)S(1)} %get-tuple-element.13, pred[3456]{0:T(1024)(128)(4,1)S(1)} %broadcast_in_dim.13), kind=kLoop, calls=%fused_computation.5 | loop fusion | flops 15924096 | bytes 15937920 | tf_op jit(solution)/shard_map/reduce_sum | solution.py:100
  99.4 4.7 %fusion.5 = bf16[3,128,384]{2,1,0:T(8,128)(2,1)S(1)} fusion(bf16[3456,3,128]{0,2,1:T(8,128)(2,1)S(1)} %bitcast.103, f32[3,384]{1,0:T(4,128)S(1)} %fusion.1, f32[3,384]{1,0:T(4,128)S(1)} %get-tuple-element.13, f32[3,3456,384]{2,1,0:T(8,128)S(1)} %get-tuple-element.14, pred[3456]{0:T(1024)(128)(4,1)S(1)} %broadcast_in_dim.13), kind=kOutput, calls=%fused_computation.18 | convolution fusion | flops 1039269888 | bytes 18887040 | tf_op jit(solution)/shard_map/thqk,khd->tqhd/dot_general | solution.py:101
  104.9 2.8 %collective-permute-start.20 = (bf16[384,384]{1,0:T(8,128)(2,1)S(1)}, bf16[384,384]{1,0:T(8,128)(2,1)S(1)}, u32[]{:S(2)}, u32[]{:S(2)}) collective-permute-start(bf16[384,384]{1,0:T(8,128)(2,1)S(1)} %convolution_convert_fusion.1), channel_id=1, source_target_pairs={{0,6},{1,7},{2,0},{3,1},{4,2},{5,3},{6,4},{7,5},{8,14},{9,15},{10,... | collective-permute-start | bytes 884744 | tf_op jit(solution)/shard_map/ppermute | solution.py:15
  108.1 2.2 %collective-permute-start.19 = (bf16[384,384]{1,0:T(8,128)(2,1)S(1)}, bf16[384,384]{1,0:T(8,128)(2,1)S(1)}, u32[]{:S(2)}, u32[]{:S(2)}) collective-permute-start(bf16[384,384]{1,0:T(8,128)(2,1)S(1)} %convolution_convert_fusion.2), channel_id=1, source_target_pairs={{0,5},{1,6},{2,7},{3,0},{4,1},{5,2},{6,3},{7,4},{8,13},{9,14},{10,... | collective-permute-start | bytes 884744 | tf_op jit(solution)/shard_map/ppermute | solution.py:15
  110.7 2.4 %collective-permute-start.18 = (bf16[384,384]{1,0:T(8,128)(2,1)S(1)}, bf16[384,384]{1,0:T(8,128)(2,1)S(1)}, u32[]{:S(2)}, u32[]{:S(2)}) collective-permute-start(bf16[384,384]{1,0:T(8,128)(2,1)S(1)} %convolution_convert_fusion.3), channel_id=1, source_target_pairs={{0,4},{1,5},{2,6},{3,7},{4,0},{5,1},{6,2},{7,3},{8,12},{9,13},{10,... | collective-permute-start | bytes 884744 | tf_op jit(solution)/shard_map/ppermute | solution.py:15
  115.5 2.3 %collective-permute-start.16 = (bf16[384,384]{1,0:T(8,128)(2,1)S(1)}, bf16[384,384]{1,0:T(8,128)(2,1)S(1)}, u32[]{:S(2)}, u32[]{:S(2)}) collective-permute-start(bf16[384,384]{1,0:T(8,128)(2,1)S(1)} %convolution_convert_fusion.5), channel_id=1, source_target_pairs={{0,2},{1,3},{2,4},{3,5},{4,6},{5,7},{6,0},{7,1},{8,10},{9,11},{10,... | collective-permute-start | bytes 884744 | tf_op jit(solution)/shard_map/ppermute | solution.py:15
  117.8 3.6 %collective-permute-start.15 = (bf16[384,384]{1,0:T(8,128)(2,1)S(1)}, bf16[384,384]{1,0:T(8,128)(2,1)S(1)}, u32[]{:S(2)}, u32[]{:S(2)}) collective-permute-start(bf16[384,384]{1,0:T(8,128)(2,1)S(1)} %convolution_convert_fusion.6), channel_id=1, source_target_pairs={{0,1},{1,2},{2,3},{3,4},{4,5},{5,6},{6,7},{7,0},{8,9},{9,10},{10,1... | collective-permute-start | bytes 884744 | tf_op jit(solution)/shard_map/ppermute | solution.py:15
  123.0 8.2 %collective-permute-done.17 = bf16[384,384]{1,0:T(8,128)(2,1)S(1)} collective-permute-done((bf16[384,384]{1,0:T(8,128)(2,1)S(1)}, bf16[384,384]{1,0:T(8,128)(2,1)S(1)}, u32[]{:S(2)}, u32[]{:S(2)}) %collective-permute-start.17) | collective-permute-done | bytes 294944 | tf_op jit(solution)/shard_map/ppermute | solution.py:15
  131.3 6.5 %collective-permute-done.16 = bf16[384,384]{1,0:T(8,128)(2,1)S(1)} collective-permute-done((bf16[384,384]{1,0:T(8,128)(2,1)S(1)}, bf16[384,384]{1,0:T(8,128)(2,1)S(1)}, u32[]{:S(2)}, u32[]{:S(2)}) %collective-permute-start.16) | collective-permute-done | bytes 294944 | tf_op jit(solution)/shard_map/ppermute | solution.py:15
  137.7 4.0 %collective-permute-done.15 = bf16[384,384]{1,0:T(8,128)(2,1)S(1)} collective-permute-done((bf16[384,384]{1,0:T(8,128)(2,1)S(1)}, bf16[384,384]{1,0:T(8,128)(2,1)S(1)}, u32[]{:S(2)}, u32[]{:S(2)}) %collective-permute-start.15) | collective-permute-done | bytes 294944 | tf_op jit(solution)/shard_map/ppermute | solution.py:15
  (82 shorter events, 40.0 us)
Async XLA Ops:
  0.0 104.1 %copy-start = (bf16[384,3072]{1,0:T(8,128)(2,1)S(1)}, bf16[384,3072]{1,0:T(8,128)(2,1)}, u32[]{:S(2)}) copy-start(bf16[384,3072]{1,0:T(8,128)(2,1)} %param.11) | copy-start | bytes 7077892
  0.0 22.9 %copy-start.4 = (bf16[384,384]{1,0:T(8,128)(2,1)S(1)}, bf16[384,384]{1,0:T(8,128)(2,1)}, u32[]{:S(2)}) copy-start(bf16[384,384]{1,0:T(8,128)(2,1)} %param.7) | copy-start | bytes 884740
  0.0 14.6 %collective-permute-start.5 = (bf16[384,384]{1,0:T(8,128)(2,1)}, bf16[384,384]{1,0:T(8,128)(2,1)}, u32[]{:S(2)}, u32[]{:S(2)}) collective-permute-start(bf16[384,384]{1,0:T(8,128)(2,1)} %param.7), channel_id=1, source_target_pairs={{0,6},{1,7},{2,0},{3,1},{4,2},{5,3},{6,4},{7,5},{8,14},{9,15},{10,... | collective-permute-start | bytes 884744 | tf_op jit(solution)/shard_map/ppermute | solution.py:15
  4.8 18.1 %collective-permute-start.4 = (bf16[384,384]{1,0:T(8,128)(2,1)}, bf16[384,384]{1,0:T(8,128)(2,1)}, u32[]{:S(2)}, u32[]{:S(2)}) collective-permute-start(bf16[384,384]{1,0:T(8,128)(2,1)} %param.7), channel_id=1, source_target_pairs={{0,5},{1,6},{2,7},{3,0},{4,1},{5,2},{6,3},{7,4},{8,13},{9,14},{10,... | collective-permute-start | bytes 884744 | tf_op jit(solution)/shard_map/ppermute | solution.py:15
  6.0 28.9 %collective-permute-start.3 = (bf16[384,384]{1,0:T(8,128)(2,1)}, bf16[384,384]{1,0:T(8,128)(2,1)S(1)}, u32[]{:S(2)}, u32[]{:S(2)}) collective-permute-start(bf16[384,384]{1,0:T(8,128)(2,1)} %param.7), channel_id=1, source_target_pairs={{0,4},{1,5},{2,6},{3,7},{4,0},{5,1},{6,2},{7,3},{8,12},{9,13},{10,... | collective-permute-start | bytes 884744 | tf_op jit(solution)/shard_map/ppermute | solution.py:15
  8.3 28.5 %collective-permute-start.2 = (bf16[384,384]{1,0:T(8,128)(2,1)}, bf16[384,384]{1,0:T(8,128)(2,1)S(1)}, u32[]{:S(2)}, u32[]{:S(2)}) collective-permute-start(bf16[384,384]{1,0:T(8,128)(2,1)} %param.7), channel_id=1, source_target_pairs={{0,3},{1,4},{2,5},{3,6},{4,7},{5,0},{6,1},{7,2},{8,11},{9,12},{10,... | collective-permute-start | bytes 884744 | tf_op jit(solution)/shard_map/ppermute | solution.py:15
  9.2 28.3 %collective-permute-start.1 = (bf16[384,384]{1,0:T(8,128)(2,1)}, bf16[384,384]{1,0:T(8,128)(2,1)S(1)}, u32[]{:S(2)}, u32[]{:S(2)}) collective-permute-start(bf16[384,384]{1,0:T(8,128)(2,1)} %param.7), channel_id=1, source_target_pairs={{0,2},{1,3},{2,4},{3,5},{4,6},{5,7},{6,0},{7,1},{8,10},{9,11},{10,... | collective-permute-start | bytes 884744 | tf_op jit(solution)/shard_map/ppermute | solution.py:15
  14.6 23.8 %collective-permute-start = (bf16[384,384]{1,0:T(8,128)(2,1)}, bf16[384,384]{1,0:T(8,128)(2,1)S(1)}, u32[]{:S(2)}, u32[]{:S(2)}) collective-permute-start(bf16[384,384]{1,0:T(8,128)(2,1)} %param.7), channel_id=1, source_target_pairs={{0,1},{1,2},{2,3},{3,4},{4,5},{5,6},{6,7},{7,0},{8,9},{9,10},{10,1... | collective-permute-start | bytes 884744 | tf_op jit(solution)/shard_map/ppermute | solution.py:15
  22.9 16.2 %collective-permute-start.6 = (bf16[384,384]{1,0:T(8,128)(2,1)S(1)}, bf16[384,384]{1,0:T(8,128)(2,1)S(1)}, u32[]{:S(2)}, u32[]{:S(2)}) collective-permute-start(bf16[384,384]{1,0:T(8,128)(2,1)S(1)} %copy-done.4), channel_id=1, source_target_pairs={{0,7},{1,0},{2,1},{3,2},{4,3},{5,4},{6,5},{7,6},{8,15},{9,8},{10,9... | collective-permute-start | bytes 884744 | tf_op jit(solution)/shard_map/ppermute | solution.py:15
  44.1 15.9 %collective-permute-start.8 = (bf16[2,384,384]{1,2,0:T(8,128)(2,1)}, bf16[2,384,384]{1,2,0:T(8,128)(2,1)}, u32[]{:S(2)}, u32[]{:S(2)}) collective-permute-start(bf16[2,384,384]{1,2,0:T(8,128)(2,1)} %get-tuple-element.11), channel_id=1, source_target_pairs={{0,16},{8,24},{16,32},{24,40},{32,48},{40,56},{48,64},{56,72},{64,... | collective-permute-start | bytes 1769480 | tf_op jit(solution)/shard_map/ppermute | solution.py:15
  45.9 15.5 %collective-permute-start.10 = (bf16[2,384,384]{1,2,0:T(8,128)(2,1)}, bf16[2,384,384]{1,2,0:T(8,128)(2,1)}, u32[]{:S(2)}, u32[]{:S(2)}) collective-permute-start(bf16[2,384,384]{1,2,0:T(8,128)(2,1)} %get-tuple-element.11), channel_id=1, source_target_pairs={{0,224},{8,232},{16,240},{24,248},{32,0},{40,8},{48,16},{56,24},{6... | collective-permute-start | bytes 1769480 | tf_op jit(solution)/shard_map/ppermute | solution.py:15
  49.9 24.9 %collective-permute-start.7 = (bf16[2,384,384]{1,2,0:T(8,128)(2,1)}, bf16[2,384,384]{1,2,0:T(8,128)(2,1)}, u32[]{:S(2)}, u32[]{:S(2)}) collective-permute-start(bf16[2,384,384]{1,2,0:T(8,128)(2,1)} %get-tuple-element.11), channel_id=1, source_target_pairs={{0,32},{8,40},{16,48},{24,56},{32,64},{40,72},{48,80},{56,88},{64,... | collective-permute-start | bytes 1769480 | tf_op jit(solution)/shard_map/ppermute | solution.py:15
  51.6 25.5 %collective-permute-start.9 = (bf16[2,384,384]{1,2,0:T(8,128)(2,1)}, bf16[2,384,384]{1,2,0:T(8,128)(2,1)}, u32[]{:S(2)}, u32[]{:S(2)}) collective-permute-start(bf16[2,384,384]{1,2,0:T(8,128)(2,1)} %get-tuple-element.11), channel_id=1, source_target_pairs={{0,240},{8,248},{16,0},{24,8},{32,16},{40,24},{48,32},{56,40},{64,... | collective-permute-start | bytes 1769480 | tf_op jit(solution)/shard_map/ppermute | solution.py:15
  53.7 30.0 %collective-permute-start.11 = (bf16[2,384,384]{1,2,0:T(8,128)(2,1)}, bf16[2,384,384]{1,2,0:T(8,128)(2,1)}, u32[]{:S(2)}, u32[]{:S(2)}) collective-permute-start(bf16[2,384,384]{1,2,0:T(8,128)(2,1)} %get-tuple-element.11), channel_id=1, source_target_pairs={{0,8},{8,0},{16,24},{24,16},{32,40},{40,32},{48,56},{56,48},{64,72... | collective-permute-start | bytes 1769480 | tf_op jit(solution)/shard_map/ppermute | solution.py:60
  60.0 25.7 %collective-permute-start.12 = (bf16[2,384,384]{1,2,0:T(8,128)(2,1)}, bf16[2,384,384]{1,2,0:T(8,128)(2,1)S(1)}, u32[]{:S(2)}, u32[]{:S(2)}) collective-permute-start(bf16[2,384,384]{1,2,0:T(8,128)(2,1)} %collective-permute-done.8), channel_id=1, source_target_pairs={{0,8},{8,0},{16,24},{24,16},{32,40},{40,32},{48,56},{56,48},{64,72... | collective-permute-start | bytes 1769480 | tf_op jit(solution)/shard_map/ppermute | solution.py:61
  77.1 10.4 %collective-permute-start.14 = (bf16[2,384,384]{1,2,0:T(8,128)(2,1)S(1)}, bf16[2,384,384]{1,2,0:T(8,128)(2,1)S(1)}, u32[]{:S(2)}, u32[]{:S(2)}) collective-permute-start(bf16[2,384,384]{1,2,0:T(8,128)(2,1)S(1)} %get-tuple-element.9), channel_id=1, source_target_pairs={{0,8},{8,0},{16,24},{24,16},{32,40},{40,32},{48,56},{56,48},{64,72... | collective-permute-start | bytes 1769480 | tf_op jit(solution)/shard_map/ppermute | solution.py:63
  77.1 9.5 %collective-permute-start.13 = (bf16[2,384,384]{1,2,0:T(8,128)(2,1)}, bf16[2,384,384]{1,2,0:T(8,128)(2,1)S(1)}, u32[]{:S(2)}, u32[]{:S(2)}) collective-permute-start(bf16[2,384,384]{1,2,0:T(8,128)(2,1)} %collective-permute-done.9), channel_id=1, source_target_pairs={{0,8},{8,0},{16,24},{24,16},{32,40},{40,32},{48,56},{56,48},{64,72... | collective-permute-start | bytes 1769480 | tf_op jit(solution)/shard_map/ppermute | solution.py:62
  104.5 11.0 %collective-permute-start.21 = (bf16[384,384]{1,0:T(8,128)(2,1)S(1)}, bf16[384,384]{1,0:T(8,128)(2,1)S(1)}, u32[]{:S(2)}, u32[]{:S(2)}) collective-permute-start(bf16[384,384]{1,0:T(8,128)(2,1)S(1)} %convolution_convert_fusion), channel_id=1, source_target_pairs={{0,7},{1,0},{2,1},{3,2},{4,3},{5,4},{6,5},{7,6},{8,15},{9,8},{10,9... | collective-permute-start | bytes 884744 | tf_op jit(solution)/shard_map/ppermute | solution.py:15
  104.9 12.8 %collective-permute-start.20 = (bf16[384,384]{1,0:T(8,128)(2,1)S(1)}, bf16[384,384]{1,0:T(8,128)(2,1)S(1)}, u32[]{:S(2)}, u32[]{:S(2)}) collective-permute-start(bf16[384,384]{1,0:T(8,128)(2,1)S(1)} %convolution_convert_fusion.1), channel_id=1, source_target_pairs={{0,6},{1,7},{2,0},{3,1},{4,2},{5,3},{6,4},{7,5},{8,14},{9,15},{10,... | collective-permute-start | bytes 884744 | tf_op jit(solution)/shard_map/ppermute | solution.py:15
  108.1 14.9 %collective-permute-start.19 = (bf16[384,384]{1,0:T(8,128)(2,1)S(1)}, bf16[384,384]{1,0:T(8,128)(2,1)S(1)}, u32[]{:S(2)}, u32[]{:S(2)}) collective-permute-start(bf16[384,384]{1,0:T(8,128)(2,1)S(1)} %convolution_convert_fusion.2), channel_id=1, source_target_pairs={{0,5},{1,6},{2,7},{3,0},{4,1},{5,2},{6,3},{7,4},{8,13},{9,14},{10,... | collective-permute-start | bytes 884744 | tf_op jit(solution)/shard_map/ppermute | solution.py:15
  110.7 12.4 %collective-permute-start.18 = (bf16[384,384]{1,0:T(8,128)(2,1)S(1)}, bf16[384,384]{1,0:T(8,128)(2,1)S(1)}, u32[]{:S(2)}, u32[]{:S(2)}) collective-permute-start(bf16[384,384]{1,0:T(8,128)(2,1)S(1)} %convolution_convert_fusion.3), channel_id=1, source_target_pairs={{0,4},{1,5},{2,6},{3,7},{4,0},{5,1},{6,2},{7,3},{8,12},{9,13},{10,... | collective-permute-start | bytes 884744 | tf_op jit(solution)/shard_map/ppermute | solution.py:15
  113.4 17.9 %collective-permute-start.17 = (bf16[384,384]{1,0:T(8,128)(2,1)S(1)}, bf16[384,384]{1,0:T(8,128)(2,1)S(1)}, u32[]{:S(2)}, u32[]{:S(2)}) collective-permute-start(bf16[384,384]{1,0:T(8,128)(2,1)S(1)} %convolution_convert_fusion.4), channel_id=1, source_target_pairs={{0,3},{1,4},{2,5},{3,6},{4,7},{5,0},{6,1},{7,2},{8,11},{9,12},{10,... | collective-permute-start | bytes 884744 | tf_op jit(solution)/shard_map/ppermute | solution.py:15
  115.5 22.3 %collective-permute-start.16 = (bf16[384,384]{1,0:T(8,128)(2,1)S(1)}, bf16[384,384]{1,0:T(8,128)(2,1)S(1)}, u32[]{:S(2)}, u32[]{:S(2)}) collective-permute-start(bf16[384,384]{1,0:T(8,128)(2,1)S(1)} %convolution_convert_fusion.5), channel_id=1, source_target_pairs={{0,2},{1,3},{2,4},{3,5},{4,6},{5,7},{6,0},{7,1},{8,10},{9,11},{10,... | collective-permute-start | bytes 884744 | tf_op jit(solution)/shard_map/ppermute | solution.py:15
  117.8 24.0 %collective-permute-start.15 = (bf16[384,384]{1,0:T(8,128)(2,1)S(1)}, bf16[384,384]{1,0:T(8,128)(2,1)S(1)}, u32[]{:S(2)}, u32[]{:S(2)}) collective-permute-start(bf16[384,384]{1,0:T(8,128)(2,1)S(1)} %convolution_convert_fusion.6), channel_id=1, source_target_pairs={{0,1},{1,2},{2,3},{3,4},{4,5},{5,6},{6,7},{7,0},{8,9},{9,10},{10,1... | collective-permute-start | bytes 884744 | tf_op jit(solution)/shard_map/ppermute | solution.py:15
  (6 other events, 58.3 us)
